TPU v7x, 128 devices: a whole 4x4x4 slice. The times are simulated.
128 devices in a mesh: redist: 32 (over x, y, core), rep: 4 (over z).
Axes of the slice: x: 4, y: 4, z: 4, core: 2. Of those that a mesh axis runs over, the one named last changes fastest.
Arguments:
- amplitudes: bfloat16 [4, 128, 1024, 1024], P(None, ('redist', 'rep')), may hold values from -6 to 6
- integrals: bfloat16 [128, 1024, 2, 1024], P(None, 'redist'), may hold values from -0.046875 to 0.046875
- occ_irrep: int32 [128], replicated, may hold values from 0 to 7, as said below
- virt_irrep: int32 [1024], replicated, may hold values from 0 to 7, as said below
Outputs:
- cycle_term: float32 [4, 1024, 2, 1024], P(None, None, None, 'redist')
Inputs may be any that keep to these rules, and one draw needn't show every extreme that they name: `occ_irrep`: labels never fall along the orbitals; each of the 8 irreps holds one contiguous range of between n // 16 and 3 * n // 16 orbitals, n being 128 or 1024. `virt_irrep`: labels never fall along the orbitals; each of the 8 irreps holds one contiguous range of between n // 16 and 3 * n // 16 orbitals, n being 128 or 1024.
All inputs are finite; a program needn't handle non-finite values.
Results may differ from a plain program's by a relative error of at most 0.0003.
Values may be sent and summed in bfloat16 or wider, within the bound.
No kernel may reach another device: no remote copies, remote signals or barrier semaphores. Data moves between devices by JAX's collectives and lax.ppermute only.
A program may use at most 192 MiB of HBM per device.

v0:
```python
import jax
import jax.numpy as jnp
from jax import lax
from jax.sharding import PartitionSpec as P

N_IRREPS = 8


def irrep_windows(virt_irrep, width):
    count = virt_irrep.shape[0]
    starts = jnp.sum(
        (virt_irrep[None, :] < jnp.arange(N_IRREPS, dtype=virt_irrep.dtype)[:, None]).astype(jnp.int32),
        axis=1,
    )
    return jnp.minimum(starts, count - width)


def parts_in(span, count):
    return min(N_IRREPS, -(-span // (count // 16)) + 1)


def shifted_pick(array, axis, width, wins, choice):
    out = None
    for g in range(N_IRREPS):
        cut = lax.dynamic_slice_in_dim(array, wins[g], width, axis=axis)
        out = cut if out is None else jnp.where(choice == g, cut, out)
    return out


def body(amplitudes, integrals, occ_irrep, virt_irrep):
    n_redist = lax.axis_size("redist")
    n_rep = lax.axis_size("rep")
    dev_index = lax.axis_index("redist")
    rep_index = lax.axis_index("rep")
    i_slab, k_block, v_width, _ = amplitudes.shape
    c_block = integrals.shape[1]
    j_slab = integrals.shape[2]
    if k_block != 1:
        raise ValueError("unsupported split")
    width = 3 * v_width // 16
    wins = irrep_windows(virt_irrep, width)
    occ_rows = occ_irrep[:i_slab]
    occ_js = occ_irrep[:j_slab]
    zero_bf = jnp.zeros((), amplitudes.dtype)

    grouped = integrals.reshape(n_redist, n_rep, k_block, c_block, j_slab, v_width)
    ints_mine = lax.dynamic_slice_in_dim(grouped, rep_index, 1, 1).reshape(
        n_redist * k_block, c_block, j_slab, v_width
    )
    moved = lax.all_to_all(ints_mine, "redist", split_axis=0, concat_axis=1, tiled=True)[0]

    k_lab = occ_irrep[dev_index * n_rep + rep_index]
    amp = amplitudes[:, 0]
    pair_ik = jnp.bitwise_xor(occ_rows, k_lab)
    per_g = []
    for g in range(N_IRREPS):
        c_irrep = jnp.bitwise_xor(g, k_lab)
        wa = wins[g]
        wc = wins[c_irrep]
        a_lab = lax.dynamic_slice_in_dim(virt_irrep, wa, width)
        cw_lab = lax.dynamic_slice_in_dim(virt_irrep, wc, width)
        a_blk = lax.dynamic_slice(amp, (0, wa, wc), (i_slab, width, width))
        allowed = pair_ik[:, None, None] == jnp.bitwise_xor(a_lab[:, None], cw_lab[None, :])[None]
        a_blk = jnp.where(allowed, a_blk, zero_bf)
        i_blk = lax.dynamic_slice(moved, (wc, 0, wa), (width, j_slab, width))
        sym = (cw_lab == c_irrep)[:, None, None] & (
            jnp.bitwise_xor(cw_lab, k_lab)[:, None, None]
            == jnp.bitwise_xor(occ_js[:, None], a_lab[None, :])[None]
        )
        i_blk = jnp.where(sym, i_blk, zero_bf)
        blk = lax.dot_general(
            i_blk, a_blk, (((0,), (2,)), ((), ())), preferred_element_type=jnp.float32
        )
        per_g.append(jnp.transpose(blk, (1, 0, 2, 3)).reshape(width, -1))
    every = jnp.concatenate(per_g, axis=0)
    b_pos = jnp.arange(v_width, dtype=jnp.int32)
    pick = virt_irrep * width + (b_pos - wins[virt_irrep])
    compact = jnp.take(every, pick, axis=0)

    n_all = n_redist * n_rep
    nb_all = v_width // n_all
    pieces = lax.all_to_all(compact.reshape(n_all, nb_all, -1), ("redist", "rep"), 0, 0, tiled=True)
    summed = jnp.sum(pieces, axis=0)
    mine_b = lax.all_gather(summed, "rep", axis=0, tiled=True)

    nb = mine_b.shape[0]
    vals = mine_b.reshape(nb, j_slab, i_slab, width).transpose(2, 3, 1, 0)
    my_b_lab = lax.dynamic_slice_in_dim(virt_irrep, dev_index * nb, nb)
    padded = jnp.pad(vals, ((0, 0), (v_width, v_width - width), (0, 0), (0, 0)))
    out = None
    for p in range(parts_in(nb, v_width)):
        lab = my_b_lab[0] + p
        start = v_width - wins[jnp.minimum(lab, N_IRREPS - 1)]
        cut = lax.dynamic_slice_in_dim(padded, start, v_width, axis=1)
        out = cut if out is None else jnp.where((my_b_lab == lab)[None, None, None, :], cut, out)
    return out


def solution(mesh):
    placed = (P(None, ("redist", "rep"), None, None), P(None, "redist", None, None), P(), P())
    return jax.shard_map(
        body, mesh=mesh, in_specs=placed, out_specs=P(None, None, None, "redist"), check_vma=False
    )
```

profile of v0, /device:TPU:6, one launch (start us, length us, event | category | flops | bytes accessed | tf_op | source)
XLA Modules:
  0.0 251.6 jit_solution(11420337884355954361)
XLA Ops:
  0.0 16.4 %copy.34 = bf16[128,32,2,1024]{3,1,2,0:T(8,128)(2,1)} copy(bf16[128,32,2,1024]{3,2,1,0:T(2,128)(2,1)} %param.5) | data formatting | bytes 33554432 | tf_op args[1]
  16.4 4.9 %dynamic-slice_bitcast_fusion = bf16[32,32,2,1024]{3,1,2,0:T(8,128)(2,1)} fusion(bf16[32,4,1,32,2,1024]{5,3,4,2,1,0:T(8,128)(2,1)} %bitcast.160, s32[]{:T(128)S(6)} %select_n.199), kind=kLoop, calls=%fused_computation.2 | loop fusion | bytes 8388612 | tf_op jit(solution)/shard_map/reshape | solution.py:47
  21.4 7.8 %all-to-all-start = ((bf16[32,32,2,1024]{3,1,2,0:T(8,128)(2,1)}), bf16[32,32,2,1024]{3,1,2,0:T(8,128)(2,1)}, u32[]{:S(2)}, u32[]{:S(2)}) async-start(bf16[32,32,2,1024]{3,1,2,0:T(8,128)(2,1)} %dynamic-slice_bitcast_fusion), calls=%async_computation | async-start | bytes 8388608 | tf_op jit(solution)/shard_map/all_to_all | solution.py:50
  29.2 0.0 copy-done.10
  29.2 0.6 dynamic_slice.158
  35.9 0.1 dynamic_slice.157
  36.8 0.1 convert_reduce_fusion
  36.9 0.7 fusion.141
  57.5 5.0 %compare_and_fusion = (pred[1024]{0:T(1024)(128)(4,1)S(1)}, s32[1024]{0:T(1024)S(1)}) fusion(s32[]{:T(128)} %bitcast.8, s32[]{:T(128)} %bitcast.7, s32[]{:T(128)} %bitcast.6, s32[]{:T(128)} %bitcast.5, s32[]{:T(128)} %bitcast.4, s32[]{:T(128)} %bitcast.3, s32[]{:T(128)} %bitcast.2, s32[]{:T(128)} %bitcast.1, s32[1024]{0:T(1024)S(1)} %copy-done.5), kind=kLoop, calls=%fused_computation.158 | loop fusion | flops 26624 | bytes 9248 | tf_op jit(solution)/shard_map/jit(_take)/and | solution.py:78
  62.5 0.7 broadcast_in_dim.42
  73.1 0.1 fusion.140
  73.2 1.4 broadcast_compare_fusion
  74.6 0.7 slice_xor_fusion
  75.3 1.3 broadcast_xor_fusion.22
  76.6 1.2 broadcast_xor_fusion.20
  77.8 1.2 broadcast_xor_fusion.18
  79.0 1.3 broadcast_xor_fusion.16
  80.2 0.6 broadcast_clamp_fusion
  80.8 0.7 broadcast_xor_fusion.8
  81.5 0.8 broadcast_xor_fusion.6
  82.3 0.9 broadcast_xor_fusion.4
  83.1 0.1 broadcast_xor_fusion.2
  83.3 0.1 broadcast_xor_fusion
  83.4 0.0 all-to-all-done
  83.4 2.6 %copy.35 = bf16[32,32,2,1024]{3,1,0,2:T(8,128)(2,1)S(1)} copy(bf16[32,32,2,1024]{3,1,2,0:T(8,128)(2,1)} %all-to-all-done) | data formatting | bytes 8388608 | tf_op jit(solution)/shard_map/all_to_all | solution.py:50
  86.0 2.1 copy-done
  88.1 1.7 fusion.2
  89.8 0.4 copy.36
  90.3 1.1 constant_dynamic-update-slice_fusion.7
  91.4 1.7 fusion.5
  93.1 0.4 copy.37
  93.6 1.8 fusion.8
  95.4 1.5 copy.38
  96.9 1.8 fusion.11
  98.7 1.5 copy.39
  100.2 1.8 fusion.14
  102.0 1.5 copy.40
  103.5 1.8 fusion.17
  105.3 1.5 copy.41
  106.8 1.8 fusion.20
  108.5 1.5 copy.42
  110.0 0.0 copy-done.8
  110.0 1.8 fusion.23
  111.8 1.5 copy.43
  113.3 1.1 constant_dynamic-update-slice_fusion.6
  114.4 2.8 %constant_dynamic-update-slice_fusion.5 = f32[1536,1536]{1,0:T(8,128)} fusion(f32[1536,1536]{1,0:T(8,128)} %constant_dynamic-update-slice_fusion.6, f32[192,1536]{1,0:T(8,128)} %copy.38), kind=kLoop, calls=%fused_computation.141 | loop fusion | bytes 2359296
  117.2 2.4 constant_dynamic-update-slice_fusion.4
  119.6 1.1 constant_dynamic-update-slice_fusion.3
  120.7 1.1 constant_dynamic-update-slice_fusion.2
  121.8 0.0 copy-done.3
  121.8 1.1 constant_dynamic-update-slice_fusion.1
  122.9 0.0 copy-done.4
  123.0 1.2 constant_dynamic-update-slice_fusion
  124.1 0.0 copy-done.7
  124.1 11.4 %gather_fusion = f32[1024,1536]{1,0:T(8,128)} fusion(f32[1536,1536]{1,0:T(8,128)} %constant_dynamic-update-slice_fusion, s32[1024]{0:T(1024)S(1)} %copy-done.7), kind=kCustom, calls=%fused_computation | custom fusion | bytes 12587008 | tf_op jit(solution)/shard_map/jit(_take)/gather | solution.py:78
  135.6 5.9 %bitcast_select_fusion = f32[128,8,1536]{2,1,0:T(8,128)} fusion(f32[1024,1536]{1,0:T(8,128)} %gather_fusion, pred[128,8]{1,0:T(8,128)(4,1)S(1)} %copy-done.6), kind=kLoop, calls=%fused_computation.1 | loop fusion | flops 1572864 | bytes 12583936 | tf_op jit(solution)/shard_map/jit(_take)/select_n | solution.py:78
  141.5 10.7 %all-to-all-start.1 = ((f32[128,8,1536]{2,1,0:T(8,128)}), f32[128,8,1536]{2,1,0:T(8,128)}, u32[]{:S(2)}, u32[]{:S(2)}) async-start(f32[128,8,1536]{2,1,0:T(8,128)} %bitcast_select_fusion), calls=%async_computation.1 | async-start | bytes 12582912 | tf_op jit(solution)/shard_map/all_to_all | solution.py:82
  154.5 0.1 broadcast_compare_fusion.8
  154.6 78.7 %all-to-all-done.1 = f32[128,8,1536]{2,1,0:T(8,128)} async-done(((f32[128,8,1536]{2,1,0:T(8,128)}), f32[128,8,1536]{2,1,0:T(8,128)}, u32[]{:S(2)}, u32[]{:S(2)}) %all-to-all-start.1) | async-done | bytes 6291488 | tf_op jit(solution)/shard_map/all_to_all | solution.py:82
  233.3 3.1 %reduce_sum.19 = f32[8,1536]{1,0:T(8,128)S(1)} reduce(f32[128,8,1536]{2,1,0:T(8,128)} %all-to-all-done.1, f32[]{:T(128)} %constant.76.clone.1), dimensions={0}, to_apply=%region_1.2 | reduce | flops 1560576 | bytes 6340612 | tf_op jit(solution)/shard_map/reduce_sum | solution.py:83
  236.5 12.1 %all_gather.3 = f32[32,1536]{1,0:T(8,128)S(1)} all-gather(f32[8,1536]{1,0:T(8,128)S(1)} %reduce_sum.19), channel_id=1, replica_groups=mesh['redist'=32,'rep'=4] {'rep'}, dimensions={0}, use_global_device_ids=true | all-gather | bytes 245760 | tf_op jit(solution)/shard_map/all_gather | solution.py:84
  248.6 0.2 reshape.516
  248.8 1.2 fusion
  250.0 1.6 copy.44
  (17 shorter events, 0.0 us)
Async XLA Ops:
  21.4 7.8 %copy-start.10 = (s32[128]{0:T(128)S(1)}, s32[128]{0:T(128)}, u32[]{:S(2)}) copy-start(s32[128]{0:T(128)} %param.6) | copy-start | bytes 1540
  21.4 14.5 %copy-start.5 = (s32[1024]{0:T(1024)S(1)}, s32[1024]{0:T(1024)}, u32[]{:S(2)}) copy-start(s32[1024]{0:T(1024)} %param.7) | copy-start | bytes 12292
  21.4 62.0 %all-to-all-start = ((bf16[32,32,2,1024]{3,1,2,0:T(8,128)(2,1)}), bf16[32,32,2,1024]{3,1,2,0:T(8,128)(2,1)}, u32[]{:S(2)}, u32[]{:S(2)}) async-start(bf16[32,32,2,1024]{3,1,2,0:T(8,128)(2,1)} %dynamic-slice_bitcast_fusion), calls=%async_computation | async-start | bytes 8388608 | tf_op jit(solution)/shard_map/all_to_all | solution.py:50
  86.0 2.1 copy-start
  102.0 8.0 %copy-start.8 = (s32[192]{0:T(256)S(1)}, s32[192]{0:T(256)}, u32[]{:S(2)}) copy-start(s32[192]{0:T(256)} %get-tuple-element.71) | copy-start | bytes 2308
  102.0 8.0 %copy-start.9 = (pred[192]{0:T(512)(128)(4,1)S(1)}, pred[192]{0:T(512)(128)(4,1)}, u32[]{:S(2)}) copy-start(pred[192]{0:T(512)(128)(4,1)} %get-tuple-element.7) | copy-start | bytes 580
  113.3 6.2 %copy-start.1 = (f32[192,1536]{1,0:T(8,128)S(1)}, f32[192,1536]{1,0:T(8,128)}, u32[]{:S(2)}) copy-start(f32[192,1536]{1,0:T(8,128)} %copy.40) | copy-start | bytes 3538948
  113.3 7.4 %copy-start.2 = (f32[192,1536]{1,0:T(8,128)S(1)}, f32[192,1536]{1,0:T(8,128)}, u32[]{:S(2)}) copy-start(f32[192,1536]{1,0:T(8,128)} %copy.41) | copy-start | bytes 3538948
  113.3 8.5 %copy-start.3 = (f32[192,1536]{1,0:T(8,128)S(1)}, f32[192,1536]{1,0:T(8,128)}, u32[]{:S(2)}) copy-start(f32[192,1536]{1,0:T(8,128)} %copy.42) | copy-start | bytes 3538948
  114.4 8.5 %copy-start.4 = (f32[192,1536]{1,0:T(8,128)S(1)}, f32[192,1536]{1,0:T(8,128)}, u32[]{:S(2)}) copy-start(f32[192,1536]{1,0:T(8,128)} %copy.43) | copy-start | bytes 3538948
  117.2 7.0 %copy-start.7 = (s32[1024]{0:T(1024)S(1)}, s32[1024]{0:T(1024)}, u32[]{:S(2)}) copy-start(s32[1024]{0:T(1024)} %broadcast_clamp_fusion) | copy-start | bytes 12292
  124.1 11.4 %copy-start.6 = (pred[128,8]{1,0:T(8,128)(4,1)S(1)}, pred[128,8]{1,0:T(8,128)(4,1)}, u32[]{:S(2)}) copy-start(pred[128,8]{1,0:T(8,128)(4,1)} %broadcast_in_dim.42) | copy-start | bytes 3076
  141.5 91.8 %all-to-all-start.1 = ((f32[128,8,1536]{2,1,0:T(8,128)}), f32[128,8,1536]{2,1,0:T(8,128)}, u32[]{:S(2)}, u32[]{:S(2)}) async-start(f32[128,8,1536]{2,1,0:T(8,128)} %bitcast_select_fusion), calls=%async_computation.1 | async-start | bytes 12582912 | tf_op jit(solution)/shard_map/all_to_all | solution.py:82
where the time goes:
time: 253 us; the launch traced here: 252 us
  waiting for transfers between devices  78.7 us (31%)
  local copies, waits for them, and re-layouts  63.3 us (25%)
  between operations  39.2 us (15%)
  other arithmetic  25.6 us (10%)
  starting transfers between devices  18.5 us (7%)
  matrix products  14.1 us (6%)
  blocking collectives  12.1 us (5%)
    all_to_all x1, waiting for transfers between devices, body(): lax.all_to_all(compact.reshape(n_all, nb_all, -1), ('redist', 'rep'), 0,...  78.7 us
    unnamed x30, local copies, waits for them, and re-layouts  29.3 us
    dot_general x8, matrix products, body(): lax.dot_general(i_blk, a_blk, (((0,), (2,)), ((), ())), preferred_element...  14.1 us
    all_gather x1, blocking collectives, body(): mine_b = lax.all_gather(summed, 'rep', axis=0, tiled=True)  12.1 us
    gather x1, local copies, waits for them, and re-layouts, body(): compact = jnp.take(every, pick, axis=0)  11.4 us
    all_to_all x1, starting transfers between devices, body(): lax.all_to_all(compact.reshape(n_all, nb_all, -1), ('redist', 'rep'), 0,...  10.7 us
    reshape x8, local copies, waits for them, and re-layouts, body(): per_g.append(jnp.transpose(blk, (1, 0, 2, 3)).reshape(width, -1))  9.8 us
    all_to_all x1, starting transfers between devices, body(): lax.all_to_all(ints_mine, 'redist', split_axis=0, concat_axis=1, tiled=True)  7.79 us
  transfers between devices with their start and end apart: 2, of which 1 were waited for; matrix products, arithmetic and copies ran while one was open for 7% of the time, Pallas kernels for 0%

commit v1 on v0

--- a/solution.py
+++ b/solution.py
@@ -47,41 +47,53 @@
     ints_mine = lax.dynamic_slice_in_dim(grouped, rep_index, 1, 1).reshape(
         n_redist * k_block, c_block, j_slab, v_width
     )
-    moved = lax.all_to_all(ints_mine, "redist", split_axis=0, concat_axis=1, tiled=True)[0]
 
     k_lab = occ_irrep[dev_index * n_rep + rep_index]
     amp = amplitudes[:, 0]
     pair_ik = jnp.bitwise_xor(occ_rows, k_lab)
-    per_g = []
+    a_blks = []
     for g in range(N_IRREPS):
-        c_irrep = jnp.bitwise_xor(g, k_lab)
         wa = wins[g]
-        wc = wins[c_irrep]
+        wc = wins[jnp.bitwise_xor(g, k_lab)]
         a_lab = lax.dynamic_slice_in_dim(virt_irrep, wa, width)
         cw_lab = lax.dynamic_slice_in_dim(virt_irrep, wc, width)
         a_blk = lax.dynamic_slice(amp, (0, wa, wc), (i_slab, width, width))
         allowed = pair_ik[:, None, None] == jnp.bitwise_xor(a_lab[:, None], cw_lab[None, :])[None]
-        a_blk = jnp.where(allowed, a_blk, zero_bf)
-        i_blk = lax.dynamic_slice(moved, (wc, 0, wa), (width, j_slab, width))
-        sym = (cw_lab == c_irrep)[:, None, None] & (
-            jnp.bitwise_xor(cw_lab, k_lab)[:, None, None]
-            == jnp.bitwise_xor(occ_js[:, None], a_lab[None, :])[None]
-        )
-        i_blk = jnp.where(sym, i_blk, zero_bf)
-        blk = lax.dot_general(
-            i_blk, a_blk, (((0,), (2,)), ((), ())), preferred_element_type=jnp.float32
-        )
-        per_g.append(jnp.transpose(blk, (1, 0, 2, 3)).reshape(width, -1))
-    every = jnp.concatenate(per_g, axis=0)
+        a_blks.append(jnp.where(allowed, a_blk, zero_bf))
+
     b_pos = jnp.arange(v_width, dtype=jnp.int32)
     pick = virt_irrep * width + (b_pos - wins[virt_irrep])
-    compact = jnp.take(every, pick, axis=0)
-
     n_all = n_redist * n_rep
     nb_all = v_width // n_all
-    pieces = lax.all_to_all(compact.reshape(n_all, nb_all, -1), ("redist", "rep"), 0, 0, tiled=True)
-    summed = jnp.sum(pieces, axis=0)
-    mine_b = lax.all_gather(summed, "rep", axis=0, tiled=True)
+    per_j = []
+    for jj in range(j_slab):
+        moved = lax.all_to_all(
+            ints_mine[:, :, jj], "redist", split_axis=0, concat_axis=1, tiled=True
+        )[0]
+        per_g = []
+        for g in range(N_IRREPS):
+            c_irrep = jnp.bitwise_xor(g, k_lab)
+            wa = wins[g]
+            wc = wins[c_irrep]
+            a_lab = lax.dynamic_slice_in_dim(virt_irrep, wa, width)
+            cw_lab = lax.dynamic_slice_in_dim(virt_irrep, wc, width)
+            i_blk = lax.dynamic_slice(moved, (wc, wa), (width, width))
+            sym = (cw_lab == c_irrep)[:, None] & (
+                jnp.bitwise_xor(cw_lab, k_lab)[:, None] == jnp.bitwise_xor(occ_js[jj], a_lab)[None, :]
+            )
+            i_blk = jnp.where(sym, i_blk, zero_bf)
+            blk = lax.dot_general(
+                i_blk, a_blks[g], (((0,), (2,)), ((), ())), preferred_element_type=jnp.float32
+            )
+            per_g.append(blk.reshape(width, -1))
+        every = jnp.concatenate(per_g, axis=0)
+        compact = jnp.take(every, pick, axis=0)
+        pieces = lax.all_to_all(
+            compact.reshape(n_all, nb_all, -1), ("redist", "rep"), 0, 0, tiled=True
+        )
+        summed = jnp.sum(pieces, axis=0)
+        per_j.append(lax.all_gather(summed, "rep", axis=0, tiled=True))
+    mine_b = jnp.stack(per_j, axis=1)
 
     nb = mine_b.shape[0]
     vals = mine_b.reshape(nb, j_slab, i_slab, width).transpose(2, 3, 1, 0)

time: 253 us -> 259 us (1.024); the launches traced: 252 us -> 254 us
  blocking collectives: 12.1 us -> 98.5 us
  waiting for transfers between devices: 78.7 us -> 0.01 us
  local copies, waits for them, and re-layouts: 63.3 us -> 35.1 us
  matrix products: 14.1 us -> 29.7 us
  other arithmetic: 25.6 us -> 30.4 us
    all_to_all x1, waiting for transfers between devices: 78.7 us -> 0.01 us  [body(): lax.all_to_all(compact.reshape(n_all, nb_all, -1), ('redist', 'rep'), 0,...]
    all_to_all x0 -> x1, blocking collectives: none -> 50.5 us  [body(): lax.all_to_all(compact.reshape(n_all, nb_all, -1), ('redist', 'rep'), 0,...]
    all_gather x1 -> x2, blocking collectives: 12.1 us -> 48 us  [body(): per_j.append(lax.all_gather(summed, 'rep', axis=0, tiled=True))]
    unnamed x30 -> x89, local copies, waits for them, and re-layouts: 29.3 us -> 1.54 us
    dot_general x8 -> x16, matrix products: 14.1 us -> 29.7 us  [body(): lax.dot_general(i_blk, a_blks[g], (((0,), (2,)), ((), ())), preferred_ele...]
    reshape x10 -> x0, local copies, waits for them, and re-layouts: 14.9 us -> none  [the longest x8 9.8 us: body(): per_g.append(jnp.transpose(blk, (1, 0, 2, 3)).reshape(width, -1))]
    dynamic_slice x2, local copies, waits for them, and re-layouts: 0.75 us -> 12.5 us  [the longest x1 6.99 us: body(): a_blk = lax.dynamic_slice(amp, (0, wa, wc), (i_slab, width, width))]
    all_to_all x1 -> x2, starting transfers between devices: 7.79 us -> 15.2 us  [body(): lax.all_to_all(ints_mine[:, :, jj], 'redist', split_axis=0, concat_axis=1...]
  transfers between devices with their start and end apart: 2 -> 3, of which waited for: 1 -> 0; matrix products, arithmetic and copies ran while one was open for 7% -> 20% of each run, Pallas kernels for 0% -> 0%
where the time goes in v1:
time: 259 us; the launch traced here: 254 us
  blocking collectives  98.5 us (38%)
  between operations  39.5 us (15%)
  local copies, waits for them, and re-layouts  35.1 us (14%)
  other arithmetic  30.4 us (12%)
  matrix products  29.7 us (11%)
  starting transfers between devices  20.7 us (8%)
    all_to_all x1, blocking collectives, body(): lax.all_to_all(compact.reshape(n_all, nb_all, -1), ('redist', 'rep'), 0,...  50.5 us
    all_gather x2, blocking collectives, body(): per_j.append(lax.all_gather(summed, 'rep', axis=0, tiled=True))  48 us
    dot_general x16, matrix products, body(): lax.dot_general(i_blk, a_blks[g], (((0,), (2,)), ((), ())), preferred_ele...  29.7 us
    all_to_all x2, starting transfers between devices, body(): lax.all_to_all(ints_mine[:, :, jj], 'redist', split_axis=0, concat_axis=1...  15.2 us
    gather x2, local copies, waits for them, and re-layouts, body(): compact = jnp.take(every, pick, axis=0)  15.1 us
    dynamic_slice x1, local copies, waits for them, and re-layouts, body(): a_blk = lax.dynamic_slice(amp, (0, wa, wc), (i_slab, width, width))  6.99 us
    xor x5, other arithmetic, body(): jnp.bitwise_xor(occ_js[jj], a_lab)[None, :]  6.16 us
    dynamic_slice x1, local copies, waits for them, and re-layouts, body(): lax.dynamic_slice_in_dim(grouped, rep_index, 1, 1)  5.56 us
  transfers between devices with their start and end apart: 3, of which 0 were waited for; matrix products, arithmetic and copies ran while one was open for 20% of the time, Pallas kernels for 0%

profile of v1, /device:TPU:6, one launch (start us, length us, event | category | flops | bytes accessed | tf_op | source)
XLA Modules:
  0.0 253.8 jit_solution(18167795695401564692)
XLA Ops:
  0.0 5.6 %constant_dynamic-slice_fusion.8 = bf16[32,1,1,32,2,1024]{5,4,3,1,0,2:T(2,128)(2,1)S(1)} fusion(bf16[32,4,1,32,2,1024]{5,4,3,1,0,2:T(2,128)(2,1)} %bitcast.115, s32[]{:T(128)S(6)} %select_n.298), kind=kLoop, calls=%fused_computation.164 | loop fusion | bytes 8388612 | tf_op jit(solution)/shard_map/dynamic_slice | solution.py:47
  5.6 1.4 copy.11
  6.9 2.4 slice_bitcast_fusion.1
  9.4 7.7 %all-to-all-start.2 = ((bf16[32,32,1024]{2,1,0:T(8,128)(2,1)}), bf16[32,32,1024]{2,1,0:T(8,128)(2,1)S(1)}, u32[]{:S(2)}, u32[]{:S(2)}) async-start(bf16[32,32,1024]{2,1,0:T(8,128)(2,1)} %get-tuple-element.49), calls=%async_computation.2 | async-start | bytes 4194304 | tf_op jit(solution)/shard_map/all_to_all | solution.py:70
  17.1 0.1 convert_reduce_fusion
  17.2 0.1 dynamic_slice.229
  17.4 0.6 fusion.109
  24.2 0.7 fusion.108
  55.0 1.3 broadcast_compare_fusion
  56.4 0.6 broadcast_xor_fusion.24
  57.0 0.6 broadcast_xor_fusion.26
  57.6 0.6 broadcast_xor_fusion.28
  58.3 0.6 broadcast_xor_fusion.30
  58.9 1.4 broadcast_xor_fusion.16
  60.3 1.2 broadcast_xor_fusion.8
  61.5 1.2 broadcast_xor_fusion.14
  62.6 0.6 slice_xor_fusion
  63.2 1.2 broadcast_xor_fusion.12
  64.5 1.2 broadcast_xor_fusion.10
  65.7 5.5 %compare_and_fusion = (pred[1024]{0:T(1024)(128)(4,1)}, s32[1024]{0:T(1024)S(1)}) fusion(s32[]{:T(128)} %bitcast.8, s32[]{:T(128)} %bitcast.7, s32[]{:T(128)} %bitcast.6, s32[]{:T(128)} %bitcast.5, s32[]{:T(128)} %bitcast.4, s32[]{:T(128)} %bitcast.3, s32[]{:T(128)} %bitcast.2, s32[]{:T(128)} %bitcast.1, s32[1024]{0:T(1024)S(1)} %copy-done.10), kind=kLoop, calls=%fused_computation.153 | loop fusion | flops 26624 | bytes 9248 | tf_op jit(solution)/shard_map/jit(_take)/and | solution.py:90
  71.2 0.8 broadcast_xor_fusion.2
  72.0 0.9 broadcast_xor_fusion.4
  72.8 0.9 broadcast_xor_fusion.6
  73.7 0.9 broadcast_xor_fusion
  74.6 0.0 all-to-all-done.2
  74.6 7.5 %all-to-all-start = ((bf16[32,32,1024]{2,1,0:T(8,128)(2,1)}), bf16[32,32,1024]{2,1,0:T(8,128)(2,1)}, u32[]{:S(2)}, u32[]{:S(2)}) async-start(bf16[32,32,1024]{2,1,0:T(8,128)(2,1)} %get-tuple-element.48), calls=%async_computation | async-start | bytes 4194304 | tf_op jit(solution)/shard_map/all_to_all | solution.py:70
  82.1 7.0 %constant_dynamic-slice_fusion = (bf16[4,1,192,192]{3,2,1,0:T(8,128)(2,1)}, bf16[4,1,192,192]{3,2,1,0:T(8,128)(2,1)}, bf16[4,1,192,192]{3,2,1,0:T(8,128)(2,1)}, ...) fusion(bf16[4,1,1024,1024]{3,2,1,0:T(8,128)(2,1)} %param.6, ...), kind=kLoop, calls=%fused_computation.156 | loop fusion | bytes 4718656 | tf_op jit(solution)/shard_map/dynamic_slice | solution.py:60
  89.1 0.1 eq.193
  89.1 0.1 eq.194
  89.3 3.1 %fusion.8 = (bf16[768,192]{1,0:T(8,128)(2,1)S(1)}, bf16[768,192]{1,0:T(8,128)(2,1)S(1)}, bf16[768,192]{1,0:T(8,128)(2,1)S(1)}, bf16[768,192]{1,0:T(8,128)(2,1)S(...) fusion(bf16[4,1,192,192]{3,2,1,0:T(8,128)(2,1)} %get-tuple-elem, ...), kind=kLoop, calls=%fused_computation.41 | loop fusion | flops 2359296 | bytes 5901312 | tf_op jit(solution)/shard_map/jit(_where)/select_n | solution.py:62
  92.5 0.0 copy-start.9
  92.5 2.0 convolution_dynamic-update-slice_fusion.7
  94.5 1.3 convolution_dynamic-update-slice_fusion.6
  95.9 1.3 convolution_dynamic-update-slice_fusion.5
  97.2 1.3 convolution_dynamic-update-slice_fusion.4
  98.5 1.3 convolution_dynamic-update-slice_fusion.3
  99.8 1.3 convolution_dynamic-update-slice_fusion.2
  101.1 1.3 convolution_dynamic-update-slice_fusion.1
  102.5 1.3 convolution_dynamic-update-slice_fusion
  103.8 6.9 %gather_fusion.1 = f32[1024,768]{1,0:T(8,128)S(1)} fusion(f32[1536,768]{1,0:T(8,128)} %convolution_dynamic-update-slice_fusion, s32[1024]{0:T(1024)S(1)} %broadcast_clamp_fusion), kind=kCustom, calls=%fused_computation.1.clone | custom fusion | bytes 6295552 | tf_op jit(solution)/shard_map/jit(_take)/gather | solution.py:90
  110.7 0.0 all-to-all-done
  110.8 2.5 convolution_dynamic-update-slice_fusion.15
  113.3 2.4 convolution_dynamic-update-slice_fusion.14
  115.7 2.4 convolution_dynamic-update-slice_fusion.13
  118.1 2.4 convolution_dynamic-update-slice_fusion.12
  120.5 2.2 convolution_dynamic-update-slice_fusion.11
  122.8 2.2 convolution_dynamic-update-slice_fusion.10
  125.0 2.2 convolution_dynamic-update-slice_fusion.9
  127.2 2.2 convolution_dynamic-update-slice_fusion.8
  129.4 8.2 %gather_fusion = f32[1024,768]{1,0:T(8,128)} fusion(f32[1536,768]{1,0:T(8,128)} %convolution_dynamic-update-slice_fusion.8, s32[1024]{0:T(1024)S(1)} %broadcast_clamp_fusion), kind=kCustom, calls=%fused_computation.clone | custom fusion | bytes 6295552 | tf_op jit(solution)/shard_map/jit(_take)/gather | solution.py:90
  137.7 4.0 %select_bitcast_fusion.1 = (f32[128,8,768]{2,1,0:T(8,128)}, f32[128,8,768]{2,1,0:T(8,128)S(1)}) fusion(f32[1024,768]{1,0:T(8,128)} %gather_fusion, pred[1024]{0:T(1024)(128)(4,1)S(1)} %copy-done.43, f32[1024,768]{1,0:T(8,128)S(1)} %gather_fusion.1), kind=kLoop, calls=%fused_computation.4 | loop fusion | flops 1572864 | bytes 12583936 | tf_op jit(solution)/shard_map/reshape | solution.py:92
  141.7 50.5 %all_to_all.28 = f32[128,8,768]{2,1,0:T(8,128)} all-to-all(f32[128,8,768]{2,1,0:T(8,128)S(1)} %get-tuple-element.87), channel_id=1, replica_groups=mesh['redist'=32,'rep'=4] {'redist','rep'}, dimensions={0} | all-to-all | bytes 6291456 | tf_op jit(solution)/shard_map/all_to_all | solution.py:91
  192.2 5.5 %all-to-all-start.1 = ((f32[128,8,768]{2,1,0:T(8,128)}), f32[128,8,768]{2,1,0:T(8,128)S(1)}, u32[]{:S(2)}, u32[]{:S(2)}) async-start(f32[128,8,768]{2,1,0:T(8,128)} %get-tuple-element.86), calls=%async_computation.1 | async-start | bytes 6291456 | tf_op jit(solution)/shard_map/all_to_all | solution.py:91
  200.3 0.1 broadcast_compare_fusion.8
  200.4 2.1 reduce_sum.29
  202.5 36.0 %all_gather.7 = f32[32,768]{1,0:T(8,128)S(1)} all-gather(f32[8,768]{1,0:T(8,128)S(1)} %reduce_sum.29), channel_id=1, replica_groups=mesh['redist'=32,'rep'=4] {'rep'}, dimensions={0}, use_global_device_ids=true | all-gather | bytes 122880 | tf_op jit(solution)/shard_map/all_gather | solution.py:95
  238.5 0.1 stack.10
  238.6 0.0 all-to-all-done.1
  238.7 0.2 reduce_sum.28
  238.9 12.0 %all_gather.6 = f32[32,768]{1,0:T(8,128)S(1)} all-gather(f32[8,768]{1,0:T(8,128)S(1)} %reduce_sum.28), channel_id=1, replica_groups=mesh['redist'=32,'rep'=4] {'rep'}, dimensions={0}, use_global_device_ids=true | all-gather | bytes 122880 | tf_op jit(solution)/shard_map/all_gather | solution.py:95
  250.8 0.1 stack.9
  251.0 0.1 maximum_bitcast_fusion
  251.1 1.2 fusion
  252.3 1.6 copy.8
  (89 shorter events, 0.2 us)
Async XLA Ops:
  9.4 7.8 %copy-start.10 = (s32[1024]{0:T(1024)S(1)}, s32[1024]{0:T(1024)}, u32[]{:S(2)}) copy-start(s32[1024]{0:T(1024)} %param.9) | copy-start | bytes 12292
  9.4 8.1 %copy-start.31 = (s32[128]{0:T(128)S(1)}, s32[128]{0:T(128)}, u32[]{:S(2)}) copy-start(s32[128]{0:T(128)} %param.8) | copy-start | bytes 1540
  9.4 65.3 %all-to-all-start.2 = ((bf16[32,32,1024]{2,1,0:T(8,128)(2,1)}), bf16[32,32,1024]{2,1,0:T(8,128)(2,1)S(1)}, u32[]{:S(2)}, u32[]{:S(2)}) async-start(bf16[32,32,1024]{2,1,0:T(8,128)(2,1)} %get-tuple-element.49), calls=%async_computation.2 | async-start | bytes 4194304 | tf_op jit(solution)/shard_map/all_to_all | solution.py:70
  57.6 40.9 %copy-start.13 = (s32[192]{0:T(256)}, s32[192]{0:T(256)S(1)}, u32[]{:S(2)}) copy-start(s32[192]{0:T(256)S(1)} %get-tuple-element.112) | copy-start | bytes 2308
  57.6 42.2 %copy-start.11 = (s32[192]{0:T(256)}, s32[192]{0:T(256)S(1)}, u32[]{:S(2)}) copy-start(s32[192]{0:T(256)S(1)} %get-tuple-element.111) | copy-start | bytes 2308
  58.2 37.6 %copy-start.16 = (s32[192]{0:T(256)}, s32[192]{0:T(256)S(1)}, u32[]{:S(2)}) copy-start(s32[192]{0:T(256)S(1)} %get-tuple-element.114) | copy-start | bytes 2308
  58.2 38.9 %copy-start.15 = (s32[192]{0:T(256)}, s32[192]{0:T(256)S(1)}, u32[]{:S(2)}) copy-start(s32[192]{0:T(256)S(1)} %get-tuple-element.113) | copy-start | bytes 2308
  58.9 33.7 %copy-start.18 = (s32[192]{0:T(256)}, s32[192]{0:T(256)S(1)}, u32[]{:S(2)}) copy-start(s32[192]{0:T(256)S(1)} %get-tuple-element.116) | copy-start | bytes 2308
  58.9 35.6 %copy-start.17 = (s32[192]{0:T(256)}, s32[192]{0:T(256)S(1)}, u32[]{:S(2)}) copy-start(s32[192]{0:T(256)S(1)} %get-tuple-element.115) | copy-start | bytes 2308
  74.6 36.1 %all-to-all-start = ((bf16[32,32,1024]{2,1,0:T(8,128)(2,1)}), bf16[32,32,1024]{2,1,0:T(8,128)(2,1)}, u32[]{:S(2)}, u32[]{:S(2)}) async-start(bf16[32,32,1024]{2,1,0:T(8,128)(2,1)} %get-tuple-element.48), calls=%async_computation | async-start | bytes 4194304 | tf_op jit(solution)/shard_map/all_to_all | solution.py:70
  89.1 3.5 %copy-start.30 = (pred[192]{0:T(512)(128)(4,1)S(1)}, pred[192]{0:T(512)(128)(4,1)}, u32[]{:S(2)}) copy-start(pred[192]{0:T(512)(128)(4,1)} %get-tuple-element.84) | copy-start | bytes 580
  89.2 5.3 %copy-start.29 = (pred[192]{0:T(512)(128)(4,1)S(1)}, pred[192]{0:T(512)(128)(4,1)}, u32[]{:S(2)}) copy-start(pred[192]{0:T(512)(128)(4,1)} %get-tuple-element.82) | copy-start | bytes 580
  89.2 5.3 %copy-start.41 = (s32[192]{0:T(256)S(1)}, s32[192]{0:T(256)}, u32[]{:S(2)}) copy-start(s32[192]{0:T(256)} %get-tuple-element.131) | copy-start | bytes 2308
  89.2 6.6 %copy-start.28 = (pred[192]{0:T(512)(128)(4,1)S(1)}, pred[192]{0:T(512)(128)(4,1)}, u32[]{:S(2)}) copy-start(pred[192]{0:T(512)(128)(4,1)} %get-tuple-element.80) | copy-start | bytes 580
  89.2 6.6 %copy-start.42 = (s32[192]{0:T(256)S(1)}, s32[192]{0:T(256)}, u32[]{:S(2)}) copy-start(s32[192]{0:T(256)} %get-tuple-element.130) | copy-start | bytes 2308
  89.2 8.0 %copy-start.27 = (pred[192]{0:T(512)(128)(4,1)S(1)}, pred[192]{0:T(512)(128)(4,1)}, u32[]{:S(2)}) copy-start(pred[192]{0:T(512)(128)(4,1)} %get-tuple-element.78) | copy-start | bytes 580
  89.2 8.0 %copy-start.40 = (s32[192]{0:T(256)S(1)}, s32[192]{0:T(256)}, u32[]{:S(2)}) copy-start(s32[192]{0:T(256)} %get-tuple-element.129) | copy-start | bytes 2308
  89.2 9.2 %copy-start.25 = (pred[192]{0:T(512)(128)(4,1)S(1)}, pred[192]{0:T(512)(128)(4,1)}, u32[]{:S(2)}) copy-start(pred[192]{0:T(512)(128)(4,1)} %get-tuple-element.76) | copy-start | bytes 580
  89.2 9.2 %copy-start.39 = (s32[192]{0:T(256)S(1)}, s32[192]{0:T(256)}, u32[]{:S(2)}) copy-start(s32[192]{0:T(256)} %get-tuple-element.128) | copy-start | bytes 2308
  92.4 10.0 %copy-start = (bf16[768,192]{1,0:T(8,128)(2,1)}, bf16[768,192]{1,0:T(8,128)(2,1)S(1)}, u32[]{:S(2)}) copy-start(bf16[768,192]{1,0:T(8,128)(2,1)S(1)} %get-tuple-element.56) | copy-start | bytes 884740
  92.4 10.0 %copy-start.2 = (bf16[768,192]{1,0:T(8,128)(2,1)}, bf16[768,192]{1,0:T(8,128)(2,1)S(1)}, u32[]{:S(2)}) copy-start(bf16[768,192]{1,0:T(8,128)(2,1)S(1)} %get-tuple-element.55) | copy-start | bytes 884740
  92.4 10.0 %copy-start.4 = (bf16[768,192]{1,0:T(8,128)(2,1)}, bf16[768,192]{1,0:T(8,128)(2,1)S(1)}, u32[]{:S(2)}) copy-start(bf16[768,192]{1,0:T(8,128)(2,1)S(1)} %get-tuple-element.54) | copy-start | bytes 884740
  92.4 10.0 %copy-start.6 = (bf16[768,192]{1,0:T(8,128)(2,1)}, bf16[768,192]{1,0:T(8,128)(2,1)S(1)}, u32[]{:S(2)}) copy-start(bf16[768,192]{1,0:T(8,128)(2,1)S(1)} %get-tuple-element.53) | copy-start | bytes 884740
  92.4 10.0 %copy-start.7 = (bf16[768,192]{1,0:T(8,128)(2,1)}, bf16[768,192]{1,0:T(8,128)(2,1)S(1)}, u32[]{:S(2)}) copy-start(bf16[768,192]{1,0:T(8,128)(2,1)S(1)} %get-tuple-element.52) | copy-start | bytes 884740
  92.4 10.0 %copy-start.8 = (bf16[768,192]{1,0:T(8,128)(2,1)}, bf16[768,192]{1,0:T(8,128)(2,1)S(1)}, u32[]{:S(2)}) copy-start(bf16[768,192]{1,0:T(8,128)(2,1)S(1)} %get-tuple-element.51) | copy-start | bytes 884740
  92.5 10.0 %copy-start.9 = (bf16[768,192]{1,0:T(8,128)(2,1)}, bf16[768,192]{1,0:T(8,128)(2,1)S(1)}, u32[]{:S(2)}) copy-start(bf16[768,192]{1,0:T(8,128)(2,1)S(1)} %get-tuple-element.57) | copy-start | bytes 884740
  92.5 7.3 %copy-start.23 = (pred[192]{0:T(512)(128)(4,1)S(1)}, pred[192]{0:T(512)(128)(4,1)}, u32[]{:S(2)}) copy-start(pred[192]{0:T(512)(128)(4,1)} %get-tuple-element.74) | copy-start | bytes 580
  92.5 7.3 %copy-start.38 = (s32[192]{0:T(256)S(1)}, s32[192]{0:T(256)}, u32[]{:S(2)}) copy-start(s32[192]{0:T(256)} %get-tuple-element.127) | copy-start | bytes 2308
  92.5 8.6 %copy-start.21 = (pred[192]{0:T(512)(128)(4,1)S(1)}, pred[192]{0:T(512)(128)(4,1)}, u32[]{:S(2)}) copy-start(pred[192]{0:T(512)(128)(4,1)} %get-tuple-element.72) | copy-start | bytes 580
  92.5 8.6 %copy-start.37 = (s32[192]{0:T(256)S(1)}, s32[192]{0:T(256)}, u32[]{:S(2)}) copy-start(s32[192]{0:T(256)} %get-tuple-element.126) | copy-start | bytes 2308
  92.5 9.9 %copy-start.19 = (pred[192]{0:T(512)(128)(4,1)S(1)}, pred[192]{0:T(512)(128)(4,1)}, u32[]{:S(2)}) copy-start(pred[192]{0:T(512)(128)(4,1)} %get-tuple-element.24) | copy-start | bytes 580
  92.5 9.9 %copy-start.36 = (s32[192]{0:T(256)S(1)}, s32[192]{0:T(256)}, u32[]{:S(2)}) copy-start(s32[192]{0:T(256)} %get-tuple-element.125) | copy-start | bytes 2308
  110.7 9.8 %copy-start.5 = (bf16[768,192]{1,0:T(8,128)(2,1)S(1)}, bf16[768,192]{1,0:T(8,128)(2,1)}, u32[]{:S(2)}) copy-start(bf16[768,192]{1,0:T(8,128)(2,1)} %copy-done.4) | copy-start | bytes 884740
  110.7 9.8 %copy-start.14 = (s32[192]{0:T(256)S(1)}, s32[192]{0:T(256)}, u32[]{:S(2)}) copy-start(s32[192]{0:T(256)} %copy-done.13) | copy-start | bytes 2308
  110.7 9.8 %copy-start.26 = (pred[192]{0:T(512)(128)(4,1)S(1)}, pred[192]{0:T(512)(128)(4,1)}, u32[]{:S(2)}) copy-start(pred[192]{0:T(512)(128)(4,1)} %get-tuple-element.76) | copy-start | bytes 580
  110.7 9.8 %copy-start.35 = (s32[192]{0:T(256)S(1)}, s32[192]{0:T(256)}, u32[]{:S(2)}) copy-start(s32[192]{0:T(256)} %get-tuple-element.64) | copy-start | bytes 2308
  110.7 12.0 %copy-start.3 = (bf16[768,192]{1,0:T(8,128)(2,1)S(1)}, bf16[768,192]{1,0:T(8,128)(2,1)}, u32[]{:S(2)}) copy-start(bf16[768,192]{1,0:T(8,128)(2,1)} %copy-done.2) | copy-start | bytes 884740
  110.7 12.0 %copy-start.12 = (s32[192]{0:T(256)S(1)}, s32[192]{0:T(256)}, u32[]{:S(2)}) copy-start(s32[192]{0:T(256)} %copy-done.11) | copy-start | bytes 2308
  110.8 12.0 %copy-start.24 = (pred[192]{0:T(512)(128)(4,1)S(1)}, pred[192]{0:T(512)(128)(4,1)}, u32[]{:S(2)}) copy-start(pred[192]{0:T(512)(128)(4,1)} %get-tuple-element.74) | copy-start | bytes 580
  110.8 12.0 %copy-start.34 = (s32[192]{0:T(256)S(1)}, s32[192]{0:T(256)}, u32[]{:S(2)}) copy-start(s32[192]{0:T(256)} %get-tuple-element.66) | copy-start | bytes 2308
  110.8 14.2 %copy-start.1 = (bf16[768,192]{1,0:T(8,128)(2,1)S(1)}, bf16[768,192]{1,0:T(8,128)(2,1)}, u32[]{:S(2)}) copy-start(bf16[768,192]{1,0:T(8,128)(2,1)} %copy-done) | copy-start | bytes 884740
  110.8 14.2 %copy-start.22 = (pred[192]{0:T(512)(128)(4,1)S(1)}, pred[192]{0:T(512)(128)(4,1)}, u32[]{:S(2)}) copy-start(pred[192]{0:T(512)(128)(4,1)} %get-tuple-element.72) | copy-start | bytes 580
  110.8 14.2 %copy-start.33 = (s32[192]{0:T(256)S(1)}, s32[192]{0:T(256)}, u32[]{:S(2)}) copy-start(s32[192]{0:T(256)} %get-tuple-element.68) | copy-start | bytes 2308
  110.8 16.4 %copy-start.20 = (pred[192]{0:T(512)(128)(4,1)S(1)}, pred[192]{0:T(512)(128)(4,1)}, u32[]{:S(2)}) copy-start(pred[192]{0:T(512)(128)(4,1)} %get-tuple-element.24) | copy-start | bytes 580
  110.8 16.4 %copy-start.32 = (s32[192]{0:T(256)S(1)}, s32[192]{0:T(256)}, u32[]{:S(2)}) copy-start(s32[192]{0:T(256)} %get-tuple-element.6) | copy-start | bytes 2308
  129.4 8.2 %copy-start.43 = (pred[1024]{0:T(1024)(128)(4,1)S(1)}, pred[1024]{0:T(1024)(128)(4,1)}, u32[]{:S(2)}) copy-start(pred[1024]{0:T(1024)(128)(4,1)} %get-tuple-element.22) | copy-start | bytes 3076
  192.2 46.5 %all-to-all-start.1 = ((f32[128,8,768]{2,1,0:T(8,128)}), f32[128,8,768]{2,1,0:T(8,128)S(1)}, u32[]{:S(2)}, u32[]{:S(2)}) async-start(f32[128,8,768]{2,1,0:T(8,128)} %get-tuple-element.86), calls=%async_computation.1 | async-start | bytes 6291456 | tf_op jit(solution)/shard_map/all_to_all | solution.py:91

commit v2 on v0

--- a/solution.py
+++ b/solution.py
@@ -52,6 +52,16 @@
     k_lab = occ_irrep[dev_index * n_rep + rep_index]
     amp = amplitudes[:, 0]
     pair_ik = jnp.bitwise_xor(occ_rows, k_lab)
+    a_blks = []
+    for g in range(N_IRREPS):
+        wa = wins[g]
+        wc = wins[jnp.bitwise_xor(g, k_lab)]
+        a_lab = lax.dynamic_slice_in_dim(virt_irrep, wa, width)
+        cw_lab = lax.dynamic_slice_in_dim(virt_irrep, wc, width)
+        a_blk = lax.dynamic_slice(amp, (0, wa, wc), (i_slab, width, width))
+        allowed = pair_ik[:, None, None] == jnp.bitwise_xor(a_lab[:, None], cw_lab[None, :])[None]
+        a_blks.append(jnp.where(allowed, a_blk, zero_bf))
+    a_blks = lax.optimization_barrier(jnp.stack(a_blks))
     per_g = []
     for g in range(N_IRREPS):
         c_irrep = jnp.bitwise_xor(g, k_lab)
@@ -59,9 +69,6 @@
         wc = wins[c_irrep]
         a_lab = lax.dynamic_slice_in_dim(virt_irrep, wa, width)
         cw_lab = lax.dynamic_slice_in_dim(virt_irrep, wc, width)
-        a_blk = lax.dynamic_slice(amp, (0, wa, wc), (i_slab, width, width))
-        allowed = pair_ik[:, None, None] == jnp.bitwise_xor(a_lab[:, None], cw_lab[None, :])[None]
-        a_blk = jnp.where(allowed, a_blk, zero_bf)
         i_blk = lax.dynamic_slice(moved, (wc, 0, wa), (width, j_slab, width))
         sym = (cw_lab == c_irrep)[:, None, None] & (
             jnp.bitwise_xor(cw_lab, k_lab)[:, None, None]
@@ -69,7 +76,7 @@
         )
         i_blk = jnp.where(sym, i_blk, zero_bf)
         blk = lax.dot_general(
-            i_blk, a_blk, (((0,), (2,)), ((), ())), preferred_element_type=jnp.float32
+            i_blk, a_blks[g], (((0,), (2,)), ((), ())), preferred_element_type=jnp.float32
         )
         per_g.append(jnp.transpose(blk, (1, 0, 2, 3)).reshape(width, -1))
     every = jnp.concatenate(per_g, axis=0)

time: 253 us -> 263 us (1.040)
  other arithmetic: 25.6 us -> 36.4 us
    unnamed x0 -> x7, other arithmetic: none -> 14.6 us
    unnamed x30 -> x24, local copies, waits for them, and re-layouts: 29.3 us -> 29 us
  transfers between devices with their start and end apart: 2 -> 2, of which waited for: 1 -> 1; matrix products, arithmetic and copies ran while one was open for 7% -> 11% of each run, Pallas kernels for 0% -> 0%
where the time goes in v2:
time: 263 us; the launch traced here: 261 us
  waiting for transfers between devices  78.6 us (30%)
  local copies, waits for them, and re-layouts  63.4 us (24%)
  between operations  39.3 us (15%)
  other arithmetic  36.4 us (14%)
  starting transfers between devices  18.4 us (7%)
  matrix products  12.7 us (5%)
  blocking collectives  12.1 us (5%)
    all_to_all x1, waiting for transfers between devices, body(): lax.all_to_all(compact.reshape(n_all, nb_all, -1), ('redist', 'rep'), 0,...  78.6 us
    unnamed x24, local copies, waits for them, and re-layouts  29 us
    unnamed x7, other arithmetic  14.6 us
    dot_general x8, matrix products, body(): lax.dot_general(i_blk, a_blks[g], (((0,), (2,)), ((), ())), preferred_ele...  12.7 us
    all_gather x1, blocking collectives, body(): mine_b = lax.all_gather(summed, 'rep', axis=0, tiled=True)  12.1 us
    gather x1, local copies, waits for them, and re-layouts, body(): compact = jnp.take(every, pick, axis=0)  11.4 us
    reshape x8, local copies, waits for them, and re-layouts, body(): per_g.append(jnp.transpose(blk, (1, 0, 2, 3)).reshape(width, -1))  10.8 us
    all_to_all x1, starting transfers between devices, body(): lax.all_to_all(compact.reshape(n_all, nb_all, -1), ('redist', 'rep'), 0,...  10.6 us
  transfers between devices with their start and end apart: 2, of which 1 were waited for; matrix products, arithmetic and copies ran while one was open for 11% of the time, Pallas kernels for 0%

profile of v2, /device:TPU:6, one launch (start us, length us, event | category | flops | bytes accessed | tf_op | source)
XLA Modules:
  0.0 261.0 jit_solution(3781392173548201413)
XLA Ops:
  0.0 16.4 %copy.34 = bf16[128,32,2,1024]{3,1,2,0:T(8,128)(2,1)} copy(bf16[128,32,2,1024]{3,2,1,0:T(2,128)(2,1)} %param.5) | data formatting | bytes 33554432 | tf_op args[1]
  16.4 4.9 %dynamic-slice_bitcast_fusion = bf16[32,32,2,1024]{3,1,2,0:T(8,128)(2,1)} fusion(bf16[32,4,1,32,2,1024]{5,3,4,2,1,0:T(8,128)(2,1)} %bitcast.144, s32[]{:T(128)S(6)} %select_n.279), kind=kLoop, calls=%fused_computation.2 | loop fusion | bytes 8388612 | tf_op jit(solution)/shard_map/reshape | solution.py:47
  21.4 7.8 %all-to-all-start = ((bf16[32,32,2,1024]{3,1,2,0:T(8,128)(2,1)}), bf16[32,32,2,1024]{3,1,2,0:T(8,128)(2,1)}, u32[]{:S(2)}, u32[]{:S(2)}) async-start(bf16[32,32,2,1024]{3,1,2,0:T(8,128)(2,1)} %dynamic-slice_bitcast_fusion), calls=%async_computation | async-start | bytes 8388608 | tf_op jit(solution)/shard_map/all_to_all | solution.py:50
  29.2 0.6 dynamic_slice.182
  35.4 0.1 convert_reduce_fusion
  36.4 0.7 fusion.93
  57.2 4.9 %compare_and_fusion = (pred[1024]{0:T(1024)(128)(4,1)S(1)}, s32[1024]{0:T(1024)S(1)}) fusion(s32[]{:T(128)} %bitcast.8, s32[]{:T(128)} %bitcast.7, s32[]{:T(128)} %bitcast.6, s32[]{:T(128)} %bitcast.5, s32[]{:T(128)} %bitcast.4, s32[]{:T(128)} %bitcast.3, s32[]{:T(128)} %bitcast.2, s32[]{:T(128)} %bitcast.1, s32[1024]{0:T(1024)S(1)} %copy-done.6), kind=kLoop, calls=%fused_computation.126 | loop fusion | flops 26624 | bytes 9248 | tf_op jit(solution)/shard_map/jit(_take)/and | solution.py:85
  72.2 0.1 fusion.92
  72.3 0.7 broadcast_compare_fusion
  73.0 0.1 broadcast_xor_fusion.2
  73.1 0.6 slice_xor_fusion
  73.7 0.1 broadcast_in_dim.41
  73.8 0.1 broadcast_xor_fusion.4
  74.0 0.1 broadcast_xor_fusion.6
  74.1 0.1 broadcast_xor_fusion
  74.2 2.0 fusion.1
  76.2 2.0 fusion.2
  78.3 2.1 fusion.3
  80.4 2.1 fusion.4
  82.5 2.1 fusion.5
  84.6 2.1 fusion.6
  86.7 2.1 fusion.7
  88.8 2.1 fusion.8
  90.9 0.6 broadcast_xor_fusion.16
  91.5 0.6 broadcast_xor_fusion.18
  92.1 0.6 broadcast_xor_fusion.20
  92.8 0.6 broadcast_xor_fusion.22
  93.4 0.1 broadcast_xor_fusion.8
  93.5 2.6 %copy.35 = bf16[32,32,2,1024]{3,1,0,2:T(8,128)(2,1)S(1)} copy(bf16[32,32,2,1024]{3,1,2,0:T(8,128)(2,1)} %all-to-all-done) | data formatting | bytes 8388608 | tf_op jit(solution)/shard_map/all_to_all | solution.py:50
  96.1 1.9 copy-done
  98.1 1.5 fusion.9
  99.6 0.4 copy.43
  100.1 1.6 fusion.10
  101.7 1.5 copy.42
  103.2 1.6 fusion.11
  104.8 1.5 copy.41
  106.3 1.6 fusion.12
  107.9 1.5 copy.40
  109.4 1.6 fusion.13
  111.0 1.5 copy.39
  112.5 1.6 fusion.14
  114.1 1.5 copy.38
  115.5 1.6 fusion.16
  117.1 1.5 copy.36
  118.6 1.6 fusion.15
  120.2 1.5 copy.37
  121.7 2.5 constant_dynamic-update-slice_fusion.7
  124.2 2.4 constant_dynamic-update-slice_fusion.6
  126.7 1.1 constant_dynamic-update-slice_fusion.5
  127.8 1.1 constant_dynamic-update-slice_fusion.4
  128.9 1.1 constant_dynamic-update-slice_fusion.3
  130.0 1.1 constant_dynamic-update-slice_fusion.2
  131.2 1.1 constant_dynamic-update-slice_fusion.1
  132.3 1.2 constant_dynamic-update-slice_fusion
  133.5 11.4 %gather_fusion = f32[1024,1536]{1,0:T(8,128)} fusion(f32[1536,1536]{1,0:T(8,128)} %constant_dynamic-update-slice_fusion, s32[1024]{0:T(1024)S(1)} %broadcast_clamp_fusion), kind=kCustom, calls=%fused_computation | custom fusion | bytes 12587008 | tf_op jit(solution)/shard_map/jit(_take)/gather | solution.py:85
  144.9 6.0 %bitcast_select_fusion = f32[128,8,1536]{2,1,0:T(8,128)} fusion(f32[1024,1536]{1,0:T(8,128)} %gather_fusion, pred[128,8]{1,0:T(8,128)(4,1)S(1)} %broadcast_in_dim.41), kind=kLoop, calls=%fused_computation.1 | loop fusion | flops 1572864 | bytes 12583936 | tf_op jit(solution)/shard_map/jit(_take)/select_n | solution.py:85
  150.8 10.6 %all-to-all-start.1 = ((f32[128,8,1536]{2,1,0:T(8,128)}), f32[128,8,1536]{2,1,0:T(8,128)}, u32[]{:S(2)}, u32[]{:S(2)}) async-start(f32[128,8,1536]{2,1,0:T(8,128)} %bitcast_select_fusion), calls=%async_computation.1 | async-start | bytes 12582912 | tf_op jit(solution)/shard_map/all_to_all | solution.py:89
  164.0 0.1 broadcast_compare_fusion.8
  164.1 78.6 %all-to-all-done.1 = f32[128,8,1536]{2,1,0:T(8,128)} async-done(((f32[128,8,1536]{2,1,0:T(8,128)}), f32[128,8,1536]{2,1,0:T(8,128)}, u32[]{:S(2)}, u32[]{:S(2)}) %all-to-all-start.1) | async-done | bytes 6291488 | tf_op jit(solution)/shard_map/all_to_all | solution.py:89
  242.7 3.1 %reduce_sum.19 = f32[8,1536]{1,0:T(8,128)S(1)} reduce(f32[128,8,1536]{2,1,0:T(8,128)} %all-to-all-done.1, f32[]{:T(128)} %constant.76.clone.1), dimensions={0}, to_apply=%region_1.2 | reduce | flops 1560576 | bytes 6340612 | tf_op jit(solution)/shard_map/reduce_sum | solution.py:90
  245.8 12.1 %all_gather.3 = f32[32,1536]{1,0:T(8,128)S(1)} all-gather(f32[8,1536]{1,0:T(8,128)S(1)} %reduce_sum.19), channel_id=1, replica_groups=mesh['redist'=32,'rep'=4] {'rep'}, dimensions={0}, use_global_device_ids=true | all-gather | bytes 245760 | tf_op jit(solution)/shard_map/all_gather | solution.py:91
  258.0 0.2 reshape.620
  258.2 1.2 fusion
  259.4 1.6 copy.44
  (19 shorter events, 0.1 us)
Async XLA Ops:
  21.4 7.8 %copy-start.7 = (s32[128]{0:T(128)S(1)}, s32[128]{0:T(128)}, u32[]{:S(2)}) copy-start(s32[128]{0:T(128)} %param.6) | copy-start | bytes 1540
  21.4 14.1 %copy-start.6 = (s32[1024]{0:T(1024)S(1)}, s32[1024]{0:T(1024)}, u32[]{:S(2)}) copy-start(s32[1024]{0:T(1024)} %param.7) | copy-start | bytes 12292
  21.4 72.1 %all-to-all-start = ((bf16[32,32,2,1024]{3,1,2,0:T(8,128)(2,1)}), bf16[32,32,2,1024]{3,1,2,0:T(8,128)(2,1)}, u32[]{:S(2)}, u32[]{:S(2)}) async-start(bf16[32,32,2,1024]{3,1,2,0:T(8,128)(2,1)} %dynamic-slice_bitcast_fusion), calls=%async_computation | async-start | bytes 8388608 | tf_op jit(solution)/shard_map/all_to_all | solution.py:50
  96.1 2.0 copy-start
  121.7 5.0 %copy-start.5 = (f32[192,1536]{1,0:T(8,128)S(1)}, f32[192,1536]{1,0:T(8,128)}, u32[]{:S(2)}) copy-start(f32[192,1536]{1,0:T(8,128)} %copy.38) | copy-start | bytes 3538948
  121.7 6.1 %copy-start.4 = (f32[192,1536]{1,0:T(8,128)S(1)}, f32[192,1536]{1,0:T(8,128)}, u32[]{:S(2)}) copy-start(f32[192,1536]{1,0:T(8,128)} %copy.39) | copy-start | bytes 3538948
  124.2 4.7 %copy-start.3 = (f32[192,1536]{1,0:T(8,128)S(1)}, f32[192,1536]{1,0:T(8,128)}, u32[]{:S(2)}) copy-start(f32[192,1536]{1,0:T(8,128)} %copy.40) | copy-start | bytes 3538948
  126.7 3.4 %copy-start.2 = (f32[192,1536]{1,0:T(8,128)S(1)}, f32[192,1536]{1,0:T(8,128)}, u32[]{:S(2)}) copy-start(f32[192,1536]{1,0:T(8,128)} %copy.41) | copy-start | bytes 3538948
  127.8 3.4 %copy-start.1 = (f32[192,1536]{1,0:T(8,128)S(1)}, f32[192,1536]{1,0:T(8,128)}, u32[]{:S(2)}) copy-start(f32[192,1536]{1,0:T(8,128)} %copy.42) | copy-start | bytes 3538948
  150.8 91.9 %all-to-all-start.1 = ((f32[128,8,1536]{2,1,0:T(8,128)}), f32[128,8,1536]{2,1,0:T(8,128)}, u32[]{:S(2)}, u32[]{:S(2)}) async-start(f32[128,8,1536]{2,1,0:T(8,128)} %bitcast_select_fusion), calls=%async_computation.1 | async-start | bytes 12582912 | tf_op jit(solution)/shard_map/all_to_all | solution.py:89

commit v3 on v0

--- a/solution.py
+++ b/solution.py
@@ -69,13 +69,14 @@
         )
         i_blk = jnp.where(sym, i_blk, zero_bf)
         blk = lax.dot_general(
-            i_blk, a_blk, (((0,), (2,)), ((), ())), preferred_element_type=jnp.float32
+            jnp.transpose(i_blk, (2, 1, 0)), a_blk, (((2,), (2,)), ((), ())),
+            preferred_element_type=jnp.float32,
         )
-        per_g.append(jnp.transpose(blk, (1, 0, 2, 3)).reshape(width, -1))
+        per_g.append(blk.reshape(width, -1))
     every = jnp.concatenate(per_g, axis=0)
     b_pos = jnp.arange(v_width, dtype=jnp.int32)
     pick = virt_irrep * width + (b_pos - wins[virt_irrep])
-    compact = jnp.take(every, pick, axis=0)
+    compact = jnp.take(every, pick, axis=0, mode="clip")
 
     n_all = n_redist * n_rep
     nb_all = v_width // n_all

time: 253 us -> 243 us (0.960)
  other arithmetic: 25.6 us -> 19.1 us
    select_n x1 -> x0, other arithmetic: 5.94 us -> none  [body(): compact = jnp.take(every, pick, axis=0)]
    gather x1, other arithmetic: 0.59 us -> 5.58 us  [body(): compact = jnp.take(every, pick, axis=0, mode='clip')]
    and x1 -> x0, other arithmetic: 4.99 us -> none  [body(): compact = jnp.take(every, pick, axis=0)]
    unnamed x30 -> x34, local copies, waits for them, and re-layouts: 29.3 us -> 27.9 us
where the time goes in v3:
time: 243 us; the launch traced here: 242 us
  waiting for transfers between devices  78.5 us (32%)
  local copies, waits for them, and re-layouts  61.2 us (25%)
  between operations  38.1 us (16%)
  other arithmetic  19.1 us (8%)
  starting transfers between devices  18.7 us (8%)
  matrix products  14.1 us (6%)
  blocking collectives  12.1 us (5%)
    all_to_all x1, waiting for transfers between devices, body(): lax.all_to_all(compact.reshape(n_all, nb_all, -1), ('redist', 'rep'), 0,...  78.5 us
    unnamed x34, local copies, waits for them, and re-layouts  27.9 us
    dot_general x8, matrix products, body(): lax.dot_general(jnp.transpose(i_blk, (2, 1, 0)), a_blk, (((2,), (2,)), ((...  14.1 us
    all_gather x1, blocking collectives, body(): mine_b = lax.all_gather(summed, 'rep', axis=0, tiled=True)  12.1 us
    gather x1, local copies, waits for them, and re-layouts, body(): compact = jnp.take(every, pick, axis=0, mode='clip')  11.4 us
    all_to_all x1, starting transfers between devices, body(): lax.all_to_all(compact.reshape(n_all, nb_all, -1), ('redist', 'rep'), 0,...  10.9 us
    reshape x8, local copies, waits for them, and re-layouts, body(): per_g.append(blk.reshape(width, -1))  9.86 us
    all_to_all x1, starting transfers between devices, body(): lax.all_to_all(ints_mine, 'redist', split_axis=0, concat_axis=1, tiled=True)  7.79 us
  transfers between devices with their start and end apart: 2, of which 1 were waited for; matrix products, arithmetic and copies ran while one was open for 7% of the time, Pallas kernels for 0%

profile of v3, /device:TPU:6, one launch (start us, length us, event | category | flops | bytes accessed | tf_op | source)
XLA Modules:
  0.0 241.8 jit_solution(13040385793861258971)
XLA Ops:
  0.0 16.4 %copy.32 = bf16[128,32,2,1024]{3,1,2,0:T(8,128)(2,1)} copy(bf16[128,32,2,1024]{3,2,1,0:T(2,128)(2,1)} %param.5) | data formatting | bytes 33554432 | tf_op args[1]
  16.4 5.0 %dynamic-slice_bitcast_fusion = bf16[32,32,2,1024]{3,1,2,0:T(8,128)(2,1)} fusion(bf16[32,4,1,32,2,1024]{5,3,4,2,1,0:T(8,128)(2,1)} %bitcast.159, s32[]{:T(128)S(6)} %select_n.187), kind=kLoop, calls=%fused_computation.1 | loop fusion | bytes 8388612 | tf_op jit(solution)/shard_map/reshape | solution.py:47
  21.4 7.8 %all-to-all-start = ((bf16[32,32,2,1024]{3,1,2,0:T(8,128)(2,1)}), bf16[32,32,2,1024]{3,1,2,0:T(8,128)(2,1)}, u32[]{:S(2)}, u32[]{:S(2)}) async-start(bf16[32,32,2,1024]{3,1,2,0:T(8,128)(2,1)} %dynamic-slice_bitcast_fusion), calls=%async_computation | async-start | bytes 8388608 | tf_op jit(solution)/shard_map/all_to_all | solution.py:50
  29.2 0.0 copy-done.12
  29.2 0.6 dynamic_slice.158
  34.9 0.0 copy-done.6
  35.0 0.1 dynamic_slice.157
  35.7 0.1 convert_reduce_fusion
  35.9 0.7 fusion.142
  66.0 0.1 fusion.141
  66.1 1.3 broadcast_compare_fusion
  67.3 0.6 slice_xor_fusion
  67.9 1.2 broadcast_xor_fusion.22
  69.1 1.1 broadcast_xor_fusion.20
  70.2 1.2 broadcast_xor_fusion.18
  71.4 1.1 broadcast_xor_fusion.16
  72.6 5.6 %fusion.130 = s32[1024]{0:T(1024)} fusion(s32[1024]{0:T(1024)S(1)} %copy-done.6, s32[]{:T(128)} %bitcast.55, s32[]{:T(128)} %bitcast.48, s32[]{:T(128)} %bitcast.41, s32[]{:T(128)} %bitcast.34, s32[]{:T(128)} %bitcast.27, s32[]{:T(128)} %bitcast.20, s32[]{:T(128)} %bitcast.13, s32[]{:T(128)} %bitcast.3), kind=kLoop, calls=%fused_computation.154 | loop fusion | flops 21504 | bytes 8224 | tf_op jit(solution)/shard_map/jit(_take)/gather | solution.py:79
  78.1 0.7 broadcast_xor_fusion.8
  78.8 0.8 broadcast_xor_fusion.6
  79.6 0.9 broadcast_xor_fusion.4
  80.4 0.1 broadcast_xor_fusion.2
  80.6 0.1 broadcast_xor_fusion
  80.7 0.0 all-to-all-done
  80.7 2.6 %copy.33 = bf16[32,32,2,1024]{3,1,0,2:T(8,128)(2,1)S(1)} copy(bf16[32,32,2,1024]{3,1,2,0:T(8,128)(2,1)} %all-to-all-done) | data formatting | bytes 8388608 | tf_op jit(solution)/shard_map/all_to_all | solution.py:50
  83.3 0.0 copy-start
  83.3 1.9 copy-done
  85.3 1.7 fusion.2
  87.0 0.4 copy.42
  87.4 1.2 constant_dynamic-update-slice_fusion.7
  88.6 1.7 fusion.5
  90.3 0.4 copy.43
  90.8 1.8 fusion.8
  92.6 1.5 copy.44
  94.2 1.8 fusion.11
  96.0 1.5 copy.45
  97.5 1.8 fusion.14
  99.3 0.0 copy-start.9
  99.3 0.0 copy-start.11
  99.3 1.5 copy.46
  100.8 1.8 fusion.17
  102.6 1.5 copy.47
  104.0 0.0 copy-done.11
  104.0 1.8 fusion.20
  105.8 1.5 copy.48
  107.3 1.8 fusion.23
  109.1 1.5 copy.49
  110.6 1.1 constant_dynamic-update-slice_fusion.6
  111.7 2.7 %constant_dynamic-update-slice_fusion.5 = f32[1536,1536]{1,0:T(8,128)} fusion(f32[1536,1536]{1,0:T(8,128)} %constant_dynamic-update-slice_fusion.6, f32[192,1536]{1,0:T(8,128)} %copy.44), kind=kLoop, calls=%fused_computation.140 | loop fusion | bytes 2359296
  114.4 1.2 constant_dynamic-update-slice_fusion.4
  115.6 1.1 constant_dynamic-update-slice_fusion.3
  116.7 1.1 constant_dynamic-update-slice_fusion.2
  117.8 1.1 constant_dynamic-update-slice_fusion.1
  118.9 0.0 copy-done.5
  118.9 1.1 constant_dynamic-update-slice_fusion
  120.0 0.0 copy-done.7
  120.0 11.4 %gather_fusion = f32[1024,1536]{1,0:T(8,128)} fusion(f32[1536,1536]{1,0:T(8,128)} %constant_dynamic-update-slice_fusion, s32[1024]{0:T(1024)S(1)} %copy-done.7), kind=kCustom, calls=%fused_computation | custom fusion | bytes 12587008 | tf_op jit(solution)/shard_map/jit(_take)/gather | solution.py:79
  131.5 10.9 %all-to-all-start.1 = ((f32[128,8,1536]{2,1,0:T(8,128)}), f32[128,8,1536]{2,1,0:T(8,128)}, u32[]{:S(2)}, u32[]{:S(2)}) async-start(f32[128,8,1536]{2,1,0:T(8,128)} %bitcast.160), calls=%async_computation.1 | async-start | bytes 12582912 | tf_op jit(solution)/shard_map/all_to_all | solution.py:83
  145.0 0.1 broadcast_compare_fusion.8
  145.1 78.5 %all-to-all-done.1 = f32[128,8,1536]{2,1,0:T(8,128)} async-done(((f32[128,8,1536]{2,1,0:T(8,128)}), f32[128,8,1536]{2,1,0:T(8,128)}, u32[]{:S(2)}, u32[]{:S(2)}) %all-to-all-start.1) | async-done | bytes 6291488 | tf_op jit(solution)/shard_map/all_to_all | solution.py:83
  223.6 3.1 %reduce_sum.19 = f32[8,1536]{1,0:T(8,128)S(1)} reduce(f32[128,8,1536]{2,1,0:T(8,128)} %all-to-all-done.1, f32[]{:T(128)} %constant.61.clone.1), dimensions={0}, to_apply=%region_1.2 | reduce | flops 1560576 | bytes 6340612 | tf_op jit(solution)/shard_map/reduce_sum | solution.py:84
  226.7 12.1 %all_gather.3 = f32[32,1536]{1,0:T(8,128)S(1)} all-gather(f32[8,1536]{1,0:T(8,128)S(1)} %reduce_sum.19), channel_id=1, replica_groups=mesh['redist'=32,'rep'=4] {'rep'}, dimensions={0}, use_global_device_ids=true | all-gather | bytes 245760 | tf_op jit(solution)/shard_map/all_gather | solution.py:85
  238.8 0.2 reshape.508
  239.1 1.2 fusion
  240.2 1.6 copy.50
  (18 shorter events, 0.0 us)
Async XLA Ops:
  21.4 7.8 %copy-start.12 = (s32[128]{0:T(128)S(1)}, s32[128]{0:T(128)}, u32[]{:S(2)}) copy-start(s32[128]{0:T(128)} %param.6) | copy-start | bytes 1540
  21.4 13.6 %copy-start.6 = (s32[1024]{0:T(1024)S(1)}, s32[1024]{0:T(1024)}, u32[]{:S(2)}) copy-start(s32[1024]{0:T(1024)} %param.7) | copy-start | bytes 12292
  21.4 59.3 %all-to-all-start = ((bf16[32,32,2,1024]{3,1,2,0:T(8,128)(2,1)}), bf16[32,32,2,1024]{3,1,2,0:T(8,128)(2,1)}, u32[]{:S(2)}, u32[]{:S(2)}) async-start(bf16[32,32,2,1024]{3,1,2,0:T(8,128)(2,1)} %dynamic-slice_bitcast_fusion), calls=%async_computation | async-start | bytes 8388608 | tf_op jit(solution)/shard_map/all_to_all | solution.py:50
  83.3 2.0 copy-start
  99.3 4.8 %copy-start.9 = (s32[192]{0:T(256)S(1)}, s32[192]{0:T(256)}, u32[]{:S(2)}) copy-start(s32[192]{0:T(256)} %get-tuple-element.70) | copy-start | bytes 2308
  99.3 4.8 %copy-start.11 = (pred[192]{0:T(512)(128)(4,1)S(1)}, pred[192]{0:T(512)(128)(4,1)}, u32[]{:S(2)}) copy-start(pred[192]{0:T(512)(128)(4,1)} %get-tuple-element.29) | copy-start | bytes 580
  102.6 4.7 %copy-start.8 = (s32[192]{0:T(256)S(1)}, s32[192]{0:T(256)}, u32[]{:S(2)}) copy-start(s32[192]{0:T(256)} %get-tuple-element.69) | copy-start | bytes 2308
  102.6 4.7 %copy-start.10 = (pred[192]{0:T(512)(128)(4,1)S(1)}, pred[192]{0:T(512)(128)(4,1)}, u32[]{:S(2)}) copy-start(pred[192]{0:T(512)(128)(4,1)} %get-tuple-element.5) | copy-start | bytes 580
  110.6 3.8 %copy-start.1 = (f32[192,1536]{1,0:T(8,128)S(1)}, f32[192,1536]{1,0:T(8,128)}, u32[]{:S(2)}) copy-start(f32[192,1536]{1,0:T(8,128)} %copy.45) | copy-start | bytes 3538948
  110.6 5.0 %copy-start.2 = (f32[192,1536]{1,0:T(8,128)S(1)}, f32[192,1536]{1,0:T(8,128)}, u32[]{:S(2)}) copy-start(f32[192,1536]{1,0:T(8,128)} %copy.46) | copy-start | bytes 3538948
  110.6 6.1 %copy-start.3 = (f32[192,1536]{1,0:T(8,128)S(1)}, f32[192,1536]{1,0:T(8,128)}, u32[]{:S(2)}) copy-start(f32[192,1536]{1,0:T(8,128)} %copy.47) | copy-start | bytes 3538948
  111.7 6.1 %copy-start.4 = (f32[192,1536]{1,0:T(8,128)S(1)}, f32[192,1536]{1,0:T(8,128)}, u32[]{:S(2)}) copy-start(f32[192,1536]{1,0:T(8,128)} %copy.48) | copy-start | bytes 3538948
  114.4 4.5 %copy-start.5 = (f32[192,1536]{1,0:T(8,128)S(1)}, f32[192,1536]{1,0:T(8,128)}, u32[]{:S(2)}) copy-start(f32[192,1536]{1,0:T(8,128)} %copy.49) | copy-start | bytes 3538948
  115.6 4.4 %copy-start.7 = (s32[1024]{0:T(1024)S(1)}, s32[1024]{0:T(1024)}, u32[]{:S(2)}) copy-start(s32[1024]{0:T(1024)} %fusion.130) | copy-start | bytes 12292
  131.5 92.1 %all-to-all-start.1 = ((f32[128,8,1536]{2,1,0:T(8,128)}), f32[128,8,1536]{2,1,0:T(8,128)}, u32[]{:S(2)}, u32[]{:S(2)}) async-start(f32[128,8,1536]{2,1,0:T(8,128)} %bitcast.160), calls=%async_computation.1 | async-start | bytes 12582912 | tf_op jit(solution)/shard_map/all_to_all | solution.py:83

commit v4 on v3

--- a/solution.py
+++ b/solution.py
@@ -47,7 +47,11 @@
     ints_mine = lax.dynamic_slice_in_dim(grouped, rep_index, 1, 1).reshape(
         n_redist * k_block, c_block, j_slab, v_width
     )
-    moved = lax.all_to_all(ints_mine, "redist", split_axis=0, concat_axis=1, tiled=True)[0]
+    dest_lab = occ_irrep[jnp.arange(n_redist, dtype=jnp.int32) * n_rep + rep_index]
+    my_c_lab = lax.dynamic_slice_in_dim(virt_irrep, dev_index * c_block, c_block)
+    b_win = jnp.bitwise_xor(dest_lab[:, None], my_c_lab[None, :])
+    packed = shifted_pick(ints_mine, 3, width, wins, b_win[:, :, None, None])
+    moved = lax.all_to_all(packed, "redist", split_axis=0, concat_axis=1, tiled=True)[0]
 
     k_lab = occ_irrep[dev_index * n_rep + rep_index]
     amp = amplitudes[:, 0]
@@ -62,7 +66,7 @@
         a_blk = lax.dynamic_slice(amp, (0, wa, wc), (i_slab, width, width))
         allowed = pair_ik[:, None, None] == jnp.bitwise_xor(a_lab[:, None], cw_lab[None, :])[None]
         a_blk = jnp.where(allowed, a_blk, zero_bf)
-        i_blk = lax.dynamic_slice(moved, (wc, 0, wa), (width, j_slab, width))
+        i_blk = lax.dynamic_slice(moved, (wc, 0, 0), (width, j_slab, width))
         sym = (cw_lab == c_irrep)[:, None, None] & (
             jnp.bitwise_xor(cw_lab, k_lab)[:, None, None]
             == jnp.bitwise_xor(occ_js[:, None], a_lab[None, :])[None]

time: 243 us -> 245 us (level)
  other arithmetic: 19.1 us -> 24.1 us
  local copies, waits for them, and re-layouts: 61.2 us -> 57.3 us
    select_n x0 -> x2, other arithmetic: none -> 6.4 us  [the longest x1 6.4 us: shifted_pick(): out = cut if out is None else jnp.where(choice == g, cut, out)]
    reshape x1 -> x0, local copies, waits for them, and re-layouts: 4.95 us -> none  [body(): lax.dynamic_slice_in_dim(grouped, rep_index, 1, 1)]
    all_to_all x1, local copies, waits for them, and re-layouts: 2.63 us -> 0.08 us  [body(): lax.all_to_all(packed, 'redist', split_axis=0, concat_axis=1, tiled=True)[0]]
    unnamed x34 -> x18, local copies, waits for them, and re-layouts: 27.9 us -> 26.7 us
  transfers between devices with their start and end apart: 2 -> 2, of which waited for: 1 -> 1; matrix products, arithmetic and copies ran while one was open for 7% -> 3% of each run, Pallas kernels for 0% -> 0%
where the time goes in v4:
time: 245 us; the launch traced here: 243 us
  waiting for transfers between devices  78.5 us (32%)
  local copies, waits for them, and re-layouts  57.3 us (23%)
  between operations  39.7 us (16%)
  other arithmetic  24.1 us (10%)
  starting transfers between devices  18.3 us (7%)
  matrix products  13 us (5%)
  blocking collectives  12.1 us (5%)
    all_to_all x1, waiting for transfers between devices, body(): lax.all_to_all(compact.reshape(n_all, nb_all, -1), ('redist', 'rep'), 0,...  78.5 us
    unnamed x18, local copies, waits for them, and re-layouts  26.7 us
    dot_general x8, matrix products, body(): lax.dot_general(jnp.transpose(i_blk, (2, 1, 0)), a_blk, (((2,), (2,)), ((...  13 us
    all_gather x1, blocking collectives, body(): mine_b = lax.all_gather(summed, 'rep', axis=0, tiled=True)  12.1 us
    reshape x8, local copies, waits for them, and re-layouts, body(): per_g.append(blk.reshape(width, -1))  11.9 us
    gather x1, local copies, waits for them, and re-layouts, body(): compact = jnp.take(every, pick, axis=0, mode='clip')  11.4 us
    all_to_all x1, starting transfers between devices, body(): lax.all_to_all(compact.reshape(n_all, nb_all, -1), ('redist', 'rep'), 0,...  10.7 us
    all_to_all x1, starting transfers between devices, body(): lax.all_to_all(packed, 'redist', split_axis=0, concat_axis=1, tiled=True)[0]  7.61 us
  transfers between devices with their start and end apart: 2, of which 1 were waited for; matrix products, arithmetic and copies ran while one was open for 3% of the time, Pallas kernels for 0%

profile of v4, /device:TPU:6, one launch (start us, length us, event | category | flops | bytes accessed | tf_op | source)
XLA Modules:
  0.0 243.0 jit_solution(9409999745739090895)
XLA Ops:
  0.0 1.3 dynamic_slice.197
  7.0 0.8 dynamic_slice.196
  7.8 0.8 convert_reduce_fusion
  9.3 0.8 fusion.149
  20.5 5.9 %pad_clamp_fusion = (s32[1024]{0:T(1024)S(1)}, s32[1024]{0:T(1024)S(1)}) fusion(s32[32]{0:T(128)S(1)} %fusion.139, s32[]{:T(128)} %bitcast.3, s32[]{:T(128)} %bitcast.18, s32[]{:T(128)} %bitcast.16, s32[]{:T(128)} %bitcast.14, s32[]{:T(128)} %bitcast.12, s32[]{:T(128)} %bitcast.10, s32[]{:T(128)} %bitcast.8, s32[]{:T(128)} %bitcast.6, s32[1024]{0:T(1024)} %param.7), kind=kLoop, calls=%fused_computation.166 | loop fusion | flops 22528 | bytes 12448 | tf_op jit(solution)/shard_map/gather | solution.py:50
  26.4 1.4 gather_fusion
  27.7 0.1 xor_compare_fusion.6
  33.1 11.2 %copy.32 = bf16[128,32,2,1024]{3,1,2,0:T(8,128)(2,1)S(1)} copy(bf16[128,32,2,1024]{3,2,1,0:T(2,128)(2,1)} %param.5) | data formatting | bytes 33554432 | tf_op args[1]
  44.2 0.0 copy-start.4
  44.2 0.0 copy-start
  44.2 6.4 %fusion.6 = bf16[32,32,2,192]{3,1,2,0:T(8,128)(2,1)} fusion(bf16[32,4,1,32,2,1024]{5,3,4,2,1,0:T(8,128)(2,1)S(1)} %bitcast.188, s32[]{:T(128)S(6)} %select_n.240, s32[]{:T(128)S(6)} %select_n.255, s32[]{:T(128)S(6)} %select_n.254, s32[]{:T(128)S(6)} %select_n.252, s32[]{:T(128)S(6)} %select_n.250, s32[]{:T(128)S(6)} %select_n.248, s32[]{:T(128)S(6)} %select_n.246, ...), kind=kLoop, calls=%fused_computation.11 | loop fusion | flops 2752512 | bytes 7085092 | tf_op jit(solution)/shard_map/jit(_where)/select_n | solution.py:26
  50.6 7.6 %all-to-all-start = ((bf16[32,32,2,192]{3,1,2,0:T(8,128)(2,1)}), bf16[32,32,2,192]{3,1,2,0:T(8,128)(2,1)S(1)}, u32[]{:S(2)}, u32[]{:S(2)}) async-start(bf16[32,32,2,192]{3,1,2,0:T(8,128)(2,1)} %fusion.6), calls=%async_computation | async-start | bytes 2097152 | tf_op jit(solution)/shard_map/all_to_all | solution.py:54
  58.3 0.0 copy-done.4
  58.3 0.1 fusion.148
  73.1 0.7 broadcast_compare_fusion
  73.9 0.6 broadcast_xor_fusion.22
  74.5 0.8 broadcast_xor_fusion.6
  75.3 0.6 broadcast_xor_fusion.20
  75.9 0.6 broadcast_xor_fusion.18
  76.6 0.6 broadcast_xor_fusion.16
  77.2 0.0 copy-done
  77.2 0.1 broadcast_xor_fusion.8
  77.3 0.6 slice_xor_fusion
  78.0 0.9 broadcast_xor_fusion.4
  78.8 0.8 broadcast_xor_fusion.2
  79.6 0.1 broadcast_xor_fusion
  79.7 0.0 all-to-all-done
  79.7 0.1 copy.33
  79.8 1.6 fusion.8
  81.4 1.5 copy.42
  82.9 2.4 constant_dynamic-update-slice_fusion.7
  85.3 1.5 fusion.11
  86.9 0.0 copy-start.3
  86.9 1.5 copy.43
  88.4 1.7 fusion.14
  90.0 1.5 copy.44
  91.5 1.7 fusion.17
  93.2 1.5 copy.45
  94.6 0.0 copy-done.3
  94.6 1.6 fusion.20
  96.3 1.5 copy.46
  97.8 1.6 fusion.23
  99.4 1.5 copy.47
  100.9 1.6 fusion.26
  102.5 1.5 copy.48
  104.0 1.6 fusion.29
  105.6 1.5 copy.49
  107.1 2.5 %constant_dynamic-update-slice_fusion.6 = f32[1536,1536]{1,0:T(8,128)} fusion(f32[1536,1536]{1,0:T(8,128)} %constant_dynamic-update-slice_fusion.7, f32[192,1536]{1,0:T(8,128)} %copy.43), kind=kLoop, calls=%fused_computation.155 | loop fusion | bytes 2359296
  109.6 2.4 constant_dynamic-update-slice_fusion.5
  112.0 2.4 constant_dynamic-update-slice_fusion.4
  114.4 2.4 constant_dynamic-update-slice_fusion.3
  116.7 0.0 copy-done.1
  116.8 1.1 constant_dynamic-update-slice_fusion.2
  117.9 2.4 constant_dynamic-update-slice_fusion.1
  120.3 1.2 constant_dynamic-update-slice_fusion
  121.5 11.4 %gather_fusion.1 = f32[1024,1536]{1,0:T(8,128)} fusion(f32[1536,1536]{1,0:T(8,128)} %constant_dynamic-update-slice_fusion, s32[1024]{0:T(1024)S(1)} %get-tuple-element.93), kind=kCustom, calls=%fused_computation.1 | custom fusion | bytes 12587008 | tf_op jit(solution)/shard_map/jit(_take)/gather | solution.py:83
  132.9 10.7 %all-to-all-start.1 = ((f32[128,8,1536]{2,1,0:T(8,128)}), f32[128,8,1536]{2,1,0:T(8,128)}, u32[]{:S(2)}, u32[]{:S(2)}) async-start(f32[128,8,1536]{2,1,0:T(8,128)} %bitcast.189), calls=%async_computation.1 | async-start | bytes 12582912 | tf_op jit(solution)/shard_map/all_to_all | solution.py:87
  146.1 0.1 broadcast_compare_fusion.8
  146.2 78.5 %all-to-all-done.1 = f32[128,8,1536]{2,1,0:T(8,128)} async-done(((f32[128,8,1536]{2,1,0:T(8,128)}), f32[128,8,1536]{2,1,0:T(8,128)}, u32[]{:S(2)}, u32[]{:S(2)}) %all-to-all-start.1) | async-done | bytes 6291488 | tf_op jit(solution)/shard_map/all_to_all | solution.py:87
  224.8 3.1 %reduce_sum.19 = f32[8,1536]{1,0:T(8,128)S(1)} reduce(f32[128,8,1536]{2,1,0:T(8,128)} %all-to-all-done.1, f32[]{:T(128)} %constant.295.clone.1), dimensions={0}, to_apply=%region_1.2 | reduce | flops 1560576 | bytes 6340612 | tf_op jit(solution)/shard_map/reduce_sum | solution.py:88
  227.9 12.1 %all_gather.3 = f32[32,1536]{1,0:T(8,128)S(1)} all-gather(f32[8,1536]{1,0:T(8,128)S(1)} %reduce_sum.19), channel_id=1, replica_groups=mesh['redist'=32,'rep'=4] {'rep'}, dimensions={0}, use_global_device_ids=true | all-gather | bytes 245760 | tf_op jit(solution)/shard_map/all_gather | solution.py:89
  240.0 0.2 reshape.705
  240.2 1.2 fusion
  241.4 1.6 copy.50
  (5 shorter events, 0.0 us)
Async XLA Ops:
  44.2 14.0 %copy-start.4 = (s32[1024]{0:T(1024)S(1)}, s32[1024]{0:T(1024)}, u32[]{:S(2)}) copy-start(s32[1024]{0:T(1024)} %param.7) | copy-start | bytes 12292
  44.2 33.0 %copy-start = (s32[128]{0:T(128)S(1)}, s32[128]{0:T(128)}, u32[]{:S(2)}) copy-start(s32[128]{0:T(128)} %param.6) | copy-start | bytes 1540
  50.6 29.1 %all-to-all-start = ((bf16[32,32,2,192]{3,1,2,0:T(8,128)(2,1)}), bf16[32,32,2,192]{3,1,2,0:T(8,128)(2,1)S(1)}, u32[]{:S(2)}, u32[]{:S(2)}) async-start(bf16[32,32,2,192]{3,1,2,0:T(8,128)(2,1)} %fusion.6), calls=%async_computation | async-start | bytes 2097152 | tf_op jit(solution)/shard_map/all_to_all | solution.py:54
  86.9 7.8 %copy-start.3 = (s32[192,192]{1,0:T(8,128)S(1)}, s32[192,192]{1,0:T(8,128)}, u32[]{:S(2)}) copy-start(s32[192,192]{1,0:T(8,128)} %get-tuple-element.87) | copy-start | bytes 442372
  107.1 9.6 %copy-start.1 = (f32[192,1536]{1,0:T(8,128)S(1)}, f32[192,1536]{1,0:T(8,128)}, u32[]{:S(2)}) copy-start(f32[192,1536]{1,0:T(8,128)} %copy.47) | copy-start | bytes 3538948
  107.1 13.2 %copy-start.2 = (f32[192,1536]{1,0:T(8,128)S(1)}, f32[192,1536]{1,0:T(8,128)}, u32[]{:S(2)}) copy-start(f32[192,1536]{1,0:T(8,128)} %copy.49) | copy-start | bytes 3538948
  132.9 91.9 %all-to-all-start.1 = ((f32[128,8,1536]{2,1,0:T(8,128)}), f32[128,8,1536]{2,1,0:T(8,128)}, u32[]{:S(2)}, u32[]{:S(2)}) async-start(f32[128,8,1536]{2,1,0:T(8,128)} %bitcast.189), calls=%async_computation.1 | async-start | bytes 12582912 | tf_op jit(solution)/shard_map/all_to_all | solution.py:87

commit v5 on v4

--- a/solution.py
+++ b/solution.py
@@ -47,7 +47,9 @@
     ints_mine = lax.dynamic_slice_in_dim(grouped, rep_index, 1, 1).reshape(
         n_redist * k_block, c_block, j_slab, v_width
     )
-    dest_lab = occ_irrep[jnp.arange(n_redist, dtype=jnp.int32) * n_rep + rep_index]
+    dest_lab = lax.dynamic_index_in_dim(
+        occ_irrep[: n_redist * n_rep].reshape(n_redist, n_rep), rep_index, 1, keepdims=False
+    )
     my_c_lab = lax.dynamic_slice_in_dim(virt_irrep, dev_index * c_block, c_block)
     b_win = jnp.bitwise_xor(dest_lab[:, None], my_c_lab[None, :])
     packed = shifted_pick(ints_mine, 3, width, wins, b_win[:, :, None, None])
@@ -79,7 +81,10 @@
         per_g.append(blk.reshape(width, -1))
     every = jnp.concatenate(per_g, axis=0)
     b_pos = jnp.arange(v_width, dtype=jnp.int32)
-    pick = virt_irrep * width + (b_pos - wins[virt_irrep])
+    b_win_start = jnp.zeros_like(virt_irrep)
+    for g in range(N_IRREPS):
+        b_win_start = jnp.where(virt_irrep == g, wins[g], b_win_start)
+    pick = virt_irrep * width + (b_pos - b_win_start)
     compact = jnp.take(every, pick, axis=0, mode="clip")
 
     n_all = n_redist * n_rep

time: 245 us -> 244 us (level)
  transfers between devices with their start and end apart: 2 -> 2, of which waited for: 1 -> 1; matrix products, arithmetic and copies ran while one was open for 3% -> 5% of each run, Pallas kernels for 0% -> 0%
where the time goes in v5:
time: 244 us; the launch traced here: 242 us
  waiting for transfers between devices  78.6 us (32%)
  local copies, waits for them, and re-layouts  56.9 us (23%)
  between operations  39.9 us (16%)
  other arithmetic  23.6 us (10%)
  starting transfers between devices  18.3 us (8%)
  matrix products  13 us (5%)
  blocking collectives  12.1 us (5%)
    all_to_all x1, waiting for transfers between devices, body(): lax.all_to_all(compact.reshape(n_all, nb_all, -1), ('redist', 'rep'), 0,...  78.6 us
    unnamed x18, local copies, waits for them, and re-layouts  26.7 us
    dot_general x8, matrix products, body(): lax.dot_general(jnp.transpose(i_blk, (2, 1, 0)), a_blk, (((2,), (2,)), ((...  13 us
    all_gather x1, blocking collectives, body(): mine_b = lax.all_gather(summed, 'rep', axis=0, tiled=True)  12.1 us
    reshape x8, local copies, waits for them, and re-layouts, body(): per_g.append(blk.reshape(width, -1))  11.9 us
    gather x1, local copies, waits for them, and re-layouts, body(): compact = jnp.take(every, pick, axis=0, mode='clip')  11.4 us
    all_to_all x1, starting transfers between devices, body(): lax.all_to_all(compact.reshape(n_all, nb_all, -1), ('redist', 'rep'), 0,...  10.7 us
    all_to_all x1, starting transfers between devices, body(): lax.all_to_all(packed, 'redist', split_axis=0, concat_axis=1, tiled=True)[0]  7.62 us
  transfers between devices with their start and end apart: 2, of which 1 were waited for; matrix products, arithmetic and copies ran while one was open for 5% of the time, Pallas kernels for 0%

profile of v5, /device:TPU:6, one launch (start us, length us, event | category | flops | bytes accessed | tf_op | source)
XLA Modules:
  0.0 242.4 jit_solution(17007022520295400035)
XLA Ops:
  0.0 1.3 dynamic_slice.203
  7.6 0.8 dynamic_slice.202
  8.4 0.8 convert_reduce_fusion
  10.0 0.7 fusion.144
  20.7 0.8 reshape.698
  26.5 0.2 dynamic-slice_reduce_fusion
  26.7 0.1 xor_compare_fusion.6
  26.8 11.2 %copy.32 = bf16[128,32,2,1024]{3,1,2,0:T(8,128)(2,1)S(1)} copy(bf16[128,32,2,1024]{3,2,1,0:T(2,128)(2,1)} %param.5) | data formatting | bytes 33554432 | tf_op args[1]
  37.9 0.0 copy-start.3
  37.9 0.0 copy-start.4
  38.0 6.4 %fusion.6 = bf16[32,32,2,192]{3,1,2,0:T(8,128)(2,1)} fusion(bf16[32,4,1,32,2,1024]{5,3,4,2,1,0:T(8,128)(2,1)S(1)} %bitcast.185, s32[]{:T(128)S(6)} %select_n.253, s32[]{:T(128)S(6)} %select_n.268, s32[]{:T(128)S(6)} %select_n.267, s32[]{:T(128)S(6)} %select_n.265, s32[]{:T(128)S(6)} %select_n.263, s32[]{:T(128)S(6)} %select_n.261, s32[]{:T(128)S(6)} %select_n.259, ...), kind=kLoop, calls=%fused_computation.10 | loop fusion | flops 2752512 | bytes 7085092 | tf_op jit(solution)/shard_map/jit(_where)/select_n | solution.py:26
  44.3 7.6 %all-to-all-start = ((bf16[32,32,2,192]{3,1,2,0:T(8,128)(2,1)}), bf16[32,32,2,192]{3,1,2,0:T(8,128)(2,1)S(1)}, u32[]{:S(2)}, u32[]{:S(2)}) async-start(bf16[32,32,2,192]{3,1,2,0:T(8,128)(2,1)} %fusion.6), calls=%async_computation | async-start | bytes 2097152 | tf_op jit(solution)/shard_map/all_to_all | solution.py:56
  52.0 0.0 copy-done.3
  52.0 0.1 fusion.143
  62.1 5.0 %add_clamp_fusion = s32[1024]{0:T(1024)S(1)} fusion(s32[1024]{0:T(1024)S(1)} %copy-done.3, s32[]{:T(128)} %bitcast.3, s32[]{:T(128)} %bitcast.17, s32[]{:T(128)} %bitcast.15, s32[]{:T(128)} %bitcast.13, s32[]{:T(128)} %bitcast.11, s32[]{:T(128)} %bitcast.9, s32[]{:T(128)} %bitcast.7, s32[]{:T(128)} %bitcast.5), kind=kLoop, calls=%fused_computation.165 | loop fusion | flops 20480 | bytes 8224 | tf_op jit(solution)/shard_map/jit(_take)/gather | solution.py:88
  72.1 0.8 broadcast_compare_fusion
  72.9 0.7 broadcast_xor_fusion.22
  73.6 0.8 broadcast_xor_fusion.6
  74.4 0.7 broadcast_xor_fusion.20
  75.1 0.7 broadcast_xor_fusion.18
  75.8 0.7 broadcast_xor_fusion.16
  76.5 0.0 copy-done.4
  76.5 0.1 broadcast_xor_fusion.8
  76.6 0.7 slice_xor_fusion
  77.2 0.9 broadcast_xor_fusion.4
  78.1 0.8 broadcast_xor_fusion.2
  78.9 0.1 broadcast_xor_fusion
  79.0 0.0 all-to-all-done
  79.0 0.1 copy.33
  79.1 1.7 fusion.8
  80.8 1.5 copy.42
  82.3 2.4 constant_dynamic-update-slice_fusion.7
  84.7 1.5 fusion.11
  86.2 0.0 copy-start.2
  86.2 1.5 copy.43
  87.8 1.7 fusion.14
  89.4 1.5 copy.44
  90.9 1.7 fusion.17
  92.6 1.5 copy.45
  94.0 0.0 copy-done.2
  94.0 1.6 fusion.20
  95.7 1.5 copy.46
  97.1 1.6 fusion.23
  98.8 1.5 copy.47
  100.3 1.6 fusion.26
  101.9 1.5 copy.48
  103.4 1.6 fusion.29
  105.0 1.5 copy.49
  106.5 2.5 %constant_dynamic-update-slice_fusion.6 = f32[1536,1536]{1,0:T(8,128)} fusion(f32[1536,1536]{1,0:T(8,128)} %constant_dynamic-update-slice_fusion.7, f32[192,1536]{1,0:T(8,128)} %copy.43), kind=kLoop, calls=%fused_computation.154 | loop fusion | bytes 2359296
  109.0 2.4 constant_dynamic-update-slice_fusion.5
  111.4 2.4 constant_dynamic-update-slice_fusion.4
  113.8 2.4 constant_dynamic-update-slice_fusion.3
  116.2 1.1 constant_dynamic-update-slice_fusion.2
  117.3 2.4 constant_dynamic-update-slice_fusion.1
  119.7 1.2 constant_dynamic-update-slice_fusion
  120.9 11.4 %gather_fusion = f32[1024,1536]{1,0:T(8,128)} fusion(f32[1536,1536]{1,0:T(8,128)} %constant_dynamic-update-slice_fusion, s32[1024]{0:T(1024)S(1)} %add_clamp_fusion), kind=kCustom, calls=%fused_computation | custom fusion | bytes 12587008 | tf_op jit(solution)/shard_map/jit(_take)/gather | solution.py:88
  132.3 10.7 %all-to-all-start.1 = ((f32[128,8,1536]{2,1,0:T(8,128)}), f32[128,8,1536]{2,1,0:T(8,128)}, u32[]{:S(2)}, u32[]{:S(2)}) async-start(f32[128,8,1536]{2,1,0:T(8,128)} %bitcast.186), calls=%async_computation.1 | async-start | bytes 12582912 | tf_op jit(solution)/shard_map/all_to_all | solution.py:92
  145.5 0.1 broadcast_compare_fusion.8
  145.6 78.6 %all-to-all-done.1 = f32[128,8,1536]{2,1,0:T(8,128)} async-done(((f32[128,8,1536]{2,1,0:T(8,128)}), f32[128,8,1536]{2,1,0:T(8,128)}, u32[]{:S(2)}, u32[]{:S(2)}) %all-to-all-start.1) | async-done | bytes 6291488 | tf_op jit(solution)/shard_map/all_to_all | solution.py:92
  224.2 3.1 %reduce_sum.19 = f32[8,1536]{1,0:T(8,128)S(1)} reduce(f32[128,8,1536]{2,1,0:T(8,128)} %all-to-all-done.1, f32[]{:T(128)} %constant.302.clone.1), dimensions={0}, to_apply=%region_1.2 | reduce | flops 1560576 | bytes 6340612 | tf_op jit(solution)/shard_map/reduce_sum | solution.py:93
  227.3 12.1 %all_gather.3 = f32[32,1536]{1,0:T(8,128)S(1)} all-gather(f32[8,1536]{1,0:T(8,128)S(1)} %reduce_sum.19), channel_id=1, replica_groups=mesh['redist'=32,'rep'=4] {'rep'}, dimensions={0}, use_global_device_ids=true | all-gather | bytes 245760 | tf_op jit(solution)/shard_map/all_gather | solution.py:94
  239.4 0.2 reshape.709
  239.6 1.2 fusion
  240.8 1.6 copy.50
  (5 shorter events, 0.0 us)
Async XLA Ops:
  37.9 14.0 %copy-start.3 = (s32[1024]{0:T(1024)S(1)}, s32[1024]{0:T(1024)}, u32[]{:S(2)}) copy-start(s32[1024]{0:T(1024)} %param.7) | copy-start | bytes 12292
  37.9 38.5 %copy-start.4 = (s32[128]{0:T(128)S(1)}, s32[128]{0:T(128)}, u32[]{:S(2)}) copy-start(s32[128]{0:T(128)} %param.6) | copy-start | bytes 1540
  44.3 34.7 %all-to-all-start = ((bf16[32,32,2,192]{3,1,2,0:T(8,128)(2,1)}), bf16[32,32,2,192]{3,1,2,0:T(8,128)(2,1)S(1)}, u32[]{:S(2)}, u32[]{:S(2)}) async-start(bf16[32,32,2,192]{3,1,2,0:T(8,128)(2,1)} %fusion.6), calls=%async_computation | async-start | bytes 2097152 | tf_op jit(solution)/shard_map/all_to_all | solution.py:56
  86.2 7.8 %copy-start.2 = (s32[192,192]{1,0:T(8,128)S(1)}, s32[192,192]{1,0:T(8,128)}, u32[]{:S(2)}) copy-start(s32[192,192]{1,0:T(8,128)} %get-tuple-element.87) | copy-start | bytes 442372
  106.5 9.7 %copy-start = (f32[192,1536]{1,0:T(8,128)S(1)}, f32[192,1536]{1,0:T(8,128)}, u32[]{:S(2)}) copy-start(f32[192,1536]{1,0:T(8,128)} %copy.47) | copy-start | bytes 3538948
  106.5 13.2 %copy-start.1 = (f32[192,1536]{1,0:T(8,128)S(1)}, f32[192,1536]{1,0:T(8,128)}, u32[]{:S(2)}) copy-start(f32[192,1536]{1,0:T(8,128)} %copy.49) | copy-start | bytes 3538948
  132.3 91.9 %all-to-all-start.1 = ((f32[128,8,1536]{2,1,0:T(8,128)}), f32[128,8,1536]{2,1,0:T(8,128)}, u32[]{:S(2)}, u32[]{:S(2)}) async-start(f32[128,8,1536]{2,1,0:T(8,128)} %bitcast.186), calls=%async_computation.1 | async-start | bytes 12582912 | tf_op jit(solution)/shard_map/all_to_all | solution.py:92

commit v6 on v5

--- a/solution.py
+++ b/solution.py
@@ -52,7 +52,18 @@
     )
     my_c_lab = lax.dynamic_slice_in_dim(virt_irrep, dev_index * c_block, c_block)
     b_win = jnp.bitwise_xor(dest_lab[:, None], my_c_lab[None, :])
-    packed = shifted_pick(ints_mine, 3, width, wins, b_win[:, :, None, None])
+    b_iota = jnp.arange(v_width, dtype=jnp.int32)
+    t_iota = jnp.arange(width, dtype=jnp.int32)
+    selector = (b_iota[None, :, None] == wins[:, None, None] + t_iota[None, None, :]).astype(
+        integrals.dtype
+    )
+    every_win = lax.dot_general(
+        ints_mine, selector, (((3,), (1,)), ((), ())), preferred_element_type=jnp.float32
+    )
+    packed = every_win[:, :, :, 0]
+    for g in range(1, N_IRREPS):
+        packed = jnp.where((b_win == g)[:, :, None, None], every_win[:, :, :, g], packed)
+    packed = packed.astype(integrals.dtype)
     moved = lax.all_to_all(packed, "redist", split_axis=0, concat_axis=1, tiled=True)[0]
 
     k_lab = occ_irrep[dev_index * n_rep + rep_index]

time: 244 us -> 241 us (0.988)
  matrix products: 13 us -> 23 us
  local copies, waits for them, and re-layouts: 56.9 us -> 49.5 us
  other arithmetic: 23.6 us -> 19 us
    unnamed x18 -> x19, local copies, waits for them, and re-layouts: 26.7 us -> 14.4 us
    dot_general x0 -> x1, matrix products: none -> 10 us  [body(): lax.dot_general(ints_mine, selector, (((3,), (1,)), ((), ())), preferred_...]
    select_n x1 -> x0, other arithmetic: 6.4 us -> none  [shifted_pick(): out = cut if out is None else jnp.where(choice == g, cut, out)]
    dynamic_slice x0 -> x1, local copies, waits for them, and re-layouts: none -> 5.57 us  [body(): lax.dynamic_slice_in_dim(grouped, rep_index, 1, 1)]
where the time goes in v6:
time: 241 us; the launch traced here: 240 us
  waiting for transfers between devices  78.6 us (33%)
  local copies, waits for them, and re-layouts  49.5 us (21%)
  between operations  39.1 us (16%)
  matrix products  23 us (10%)
  other arithmetic  19 us (8%)
  starting transfers between devices  18.3 us (8%)
  blocking collectives  12.1 us (5%)
    all_to_all x1, waiting for transfers between devices, body(): lax.all_to_all(compact.reshape(n_all, nb_all, -1), ('redist', 'rep'), 0,...  78.6 us
    unnamed x19, local copies, waits for them, and re-layouts  14.4 us
    dot_general x8, matrix products, body(): lax.dot_general(jnp.transpose(i_blk, (2, 1, 0)), a_blk, (((2,), (2,)), ((...  13 us
    all_gather x1, blocking collectives, body(): mine_b = lax.all_gather(summed, 'rep', axis=0, tiled=True)  12.1 us
    reshape x8, local copies, waits for them, and re-layouts, body(): per_g.append(blk.reshape(width, -1))  11.9 us
    gather x1, local copies, waits for them, and re-layouts, body(): compact = jnp.take(every, pick, axis=0, mode='clip')  11.4 us
    all_to_all x1, starting transfers between devices, body(): lax.all_to_all(compact.reshape(n_all, nb_all, -1), ('redist', 'rep'), 0,...  10.6 us
    dot_general x1, matrix products, body(): lax.dot_general(ints_mine, selector, (((3,), (1,)), ((), ())), preferred_...  10 us
  transfers between devices with their start and end apart: 2, of which 1 were waited for; matrix products, arithmetic and copies ran while one was open for 5% of the time, Pallas kernels for 0%

profile of v6, /device:TPU:6, one launch (start us, length us, event | category | flops | bytes accessed | tf_op | source)
XLA Modules:
  0.0 239.6 jit_solution(2281251486228490987)
XLA Ops:
  0.0 0.8 convert_reduce_fusion
  0.8 0.8 dynamic_slice.164
  1.6 0.7 reshape.710
  2.3 0.2 dynamic-slice_reduce_fusion
  2.5 5.6 %constant_dynamic-slice_fusion = bf16[32,1,1,32,2,1024]{5,4,3,1,0,2:T(2,128)(2,1)S(1)} fusion(bf16[32,4,1,32,2,1024]{5,4,3,1,0,2:T(2,128)(2,1)} %bitcast.246, s32[]{:T(128)S(6)} %select_n.226), kind=kLoop, calls=%fused_computation.180 | loop fusion | bytes 8388612 | tf_op jit(solution)/shard_map/dynamic_slice | solution.py:47
  8.1 0.1 iota_add_fusion
  8.2 0.1 xor_compare_fusion.6
  8.2 10.0 %fusion.1 = bf16[32,32,2,8,192]{4,1,3,2,0:T(8,128)(2,1)S(1)} fusion(bf16[32,1,1,32,2,1024]{5,4,3,1,0,2:T(2,128)(2,1)S(1)} %constant_dynamic-slice_fusion, s32[8,192]{1,0:T(8,128)S(1)} %iota_add_fusion), kind=kOutput, calls=%fused_computation.3 | convolution fusion | flops 6444023808 | bytes 10491904 | tf_op jit(solution)/shard_map/dot_general | solution.py:60
  18.3 0.0 copy-start.5
  18.3 0.0 copy-start.4
  18.3 2.4 fusion.11
  20.6 7.6 %all-to-all-start = ((bf16[32,32,2,192]{3,1,2,0:T(8,128)(2,1)}), bf16[32,32,2,192]{3,1,2,0:T(8,128)(2,1)S(1)}, u32[]{:S(2)}, u32[]{:S(2)}) async-start(bf16[32,32,2,192]{3,1,2,0:T(8,128)(2,1)} %fusion.11), calls=%async_computation | async-start | bytes 2097152 | tf_op jit(solution)/shard_map/all_to_all | solution.py:67
  28.3 0.0 copy-done.5
  28.3 0.6 dynamic_slice.165
  34.7 0.7 fusion.150
  55.8 0.0 copy-done.4
  55.8 5.1 %add_clamp_fusion = s32[1024]{0:T(1024)S(1)} fusion(s32[1024]{0:T(1024)S(1)} %copy-done.4, s32[]{:T(128)} %bitcast.3, s32[]{:T(128)} %bitcast.25, s32[]{:T(128)} %bitcast.32, s32[]{:T(128)} %bitcast.39, s32[]{:T(128)} %bitcast.46, s32[]{:T(128)} %bitcast.53, s32[]{:T(128)} %bitcast.60, s32[]{:T(128)} %bitcast.67), kind=kLoop, calls=%fused_computation.181 | loop fusion | flops 20480 | bytes 8224 | tf_op jit(solution)/shard_map/jit(_take)/gather | solution.py:99
  71.0 0.7 broadcast_compare_fusion
  71.7 0.6 broadcast_xor_fusion.22
  72.3 0.1 fusion.149
  72.4 0.8 broadcast_xor_fusion.6
  73.2 0.6 broadcast_xor_fusion.20
  73.7 0.6 broadcast_xor_fusion.18
  74.3 0.6 broadcast_xor_fusion.16
  74.9 0.1 broadcast_xor_fusion.8
  75.0 0.6 slice_xor_fusion
  75.6 0.9 broadcast_xor_fusion.4
  76.5 0.8 broadcast_xor_fusion.2
  77.2 0.1 broadcast_xor_fusion
  77.4 0.0 all-to-all-done
  77.4 0.1 copy.55
  77.5 1.7 fusion.14
  79.1 1.5 copy.64
  80.6 2.4 constant_dynamic-update-slice_fusion.7
  83.0 1.6 fusion.17
  84.6 1.5 copy.65
  86.2 1.6 fusion.20
  87.8 1.5 copy.66
  89.2 1.6 fusion.23
  90.8 1.5 copy.67
  92.3 1.6 fusion.26
  93.9 1.5 copy.68
  95.4 1.6 fusion.29
  97.0 1.5 copy.69
  98.5 1.6 fusion.32
  100.2 1.5 copy.70
  101.7 1.6 fusion.35
  103.3 1.5 copy.71
  104.8 2.5 %constant_dynamic-update-slice_fusion.6 = f32[1536,1536]{1,0:T(8,128)} fusion(f32[1536,1536]{1,0:T(8,128)} %constant_dynamic-update-slice_fusion.7, f32[192,1536]{1,0:T(8,128)} %copy.65), kind=kLoop, calls=%fused_computation.168 | loop fusion | bytes 2359296
  107.3 2.5 %constant_dynamic-update-slice_fusion.5 = f32[1536,1536]{1,0:T(8,128)} fusion(f32[1536,1536]{1,0:T(8,128)} %constant_dynamic-update-slice_fusion.6, f32[192,1536]{1,0:T(8,128)} %copy.66), kind=kLoop, calls=%fused_computation.167 | loop fusion | bytes 2359296
  109.8 2.4 constant_dynamic-update-slice_fusion.4
  112.1 1.1 constant_dynamic-update-slice_fusion.3
  113.3 2.4 %constant_dynamic-update-slice_fusion.2 = f32[1536,1536]{1,0:T(8,128)} fusion(f32[1536,1536]{1,0:T(8,128)} %constant_dynamic-update-slice_fusion.3, f32[192,1536]{1,0:T(8,128)} %copy.69), kind=kLoop, calls=%fused_computation.164 | loop fusion | bytes 2359296
  115.7 1.1 constant_dynamic-update-slice_fusion.1
  116.8 1.2 constant_dynamic-update-slice_fusion
  118.0 11.4 %gather_fusion = f32[1024,1536]{1,0:T(8,128)} fusion(f32[1536,1536]{1,0:T(8,128)} %constant_dynamic-update-slice_fusion, s32[1024]{0:T(1024)S(1)} %add_clamp_fusion), kind=kCustom, calls=%fused_computation | custom fusion | bytes 12587008 | tf_op jit(solution)/shard_map/jit(_take)/gather | solution.py:99
  129.4 10.6 %all-to-all-start.1 = ((f32[128,8,1536]{2,1,0:T(8,128)}), f32[128,8,1536]{2,1,0:T(8,128)}, u32[]{:S(2)}, u32[]{:S(2)}) async-start(f32[128,8,1536]{2,1,0:T(8,128)} %bitcast.229), calls=%async_computation.1 | async-start | bytes 12582912 | tf_op jit(solution)/shard_map/all_to_all | solution.py:103
  142.6 0.1 broadcast_compare_fusion.8
  142.7 78.6 %all-to-all-done.1 = f32[128,8,1536]{2,1,0:T(8,128)} async-done(((f32[128,8,1536]{2,1,0:T(8,128)}), f32[128,8,1536]{2,1,0:T(8,128)}, u32[]{:S(2)}, u32[]{:S(2)}) %all-to-all-start.1) | async-done | bytes 6291488 | tf_op jit(solution)/shard_map/all_to_all | solution.py:103
  221.3 3.1 %reduce_sum.19 = f32[8,1536]{1,0:T(8,128)S(1)} reduce(f32[128,8,1536]{2,1,0:T(8,128)} %all-to-all-done.1, f32[]{:T(128)} %constant.78.clone.1), dimensions={0}, to_apply=%region_1.2 | reduce | flops 1560576 | bytes 6340612 | tf_op jit(solution)/shard_map/reduce_sum | solution.py:104
  224.4 12.1 %all_gather.3 = f32[32,1536]{1,0:T(8,128)S(1)} all-gather(f32[8,1536]{1,0:T(8,128)S(1)} %reduce_sum.19), channel_id=1, replica_groups=mesh['redist'=32,'rep'=4] {'rep'}, dimensions={0}, use_global_device_ids=true | all-gather | bytes 245760 | tf_op jit(solution)/shard_map/all_gather | solution.py:105
  236.6 0.2 reshape.722
  236.8 1.2 fusion.12
  238.0 1.6 copy.72
  (9 shorter events, 0.0 us)
Async XLA Ops:
  18.3 10.0 %copy-start.5 = (s32[128]{0:T(128)S(1)}, s32[128]{0:T(128)}, u32[]{:S(2)}) copy-start(s32[128]{0:T(128)} %param.6) | copy-start | bytes 1540
  18.3 37.5 %copy-start.4 = (s32[1024]{0:T(1024)S(1)}, s32[1024]{0:T(1024)}, u32[]{:S(2)}) copy-start(s32[1024]{0:T(1024)} %param.7) | copy-start | bytes 12292
  20.6 56.7 %all-to-all-start = ((bf16[32,32,2,192]{3,1,2,0:T(8,128)(2,1)}), bf16[32,32,2,192]{3,1,2,0:T(8,128)(2,1)S(1)}, u32[]{:S(2)}, u32[]{:S(2)}) async-start(bf16[32,32,2,192]{3,1,2,0:T(8,128)(2,1)} %fusion.11), calls=%async_computation | async-start | bytes 2097152 | tf_op jit(solution)/shard_map/all_to_all | solution.py:67
  84.6 7.7 %copy-start.3 = (s32[192,192]{1,0:T(8,128)S(1)}, s32[192,192]{1,0:T(8,128)}, u32[]{:S(2)}) copy-start(s32[192,192]{1,0:T(8,128)} %get-tuple-element.87) | copy-start | bytes 442372
  104.8 7.4 %copy-start = (f32[192,1536]{1,0:T(8,128)S(1)}, f32[192,1536]{1,0:T(8,128)}, u32[]{:S(2)}) copy-start(f32[192,1536]{1,0:T(8,128)} %copy.68) | copy-start | bytes 3538948
  104.8 10.9 %copy-start.1 = (f32[192,1536]{1,0:T(8,128)S(1)}, f32[192,1536]{1,0:T(8,128)}, u32[]{:S(2)}) copy-start(f32[192,1536]{1,0:T(8,128)} %copy.70) | copy-start | bytes 3538948
  107.3 9.5 %copy-start.2 = (f32[192,1536]{1,0:T(8,128)S(1)}, f32[192,1536]{1,0:T(8,128)}, u32[]{:S(2)}) copy-start(f32[192,1536]{1,0:T(8,128)} %copy.71) | copy-start | bytes 3538948
  129.4 91.9 %all-to-all-start.1 = ((f32[128,8,1536]{2,1,0:T(8,128)}), f32[128,8,1536]{2,1,0:T(8,128)}, u32[]{:S(2)}, u32[]{:S(2)}) async-start(f32[128,8,1536]{2,1,0:T(8,128)} %bitcast.229), calls=%async_computation.1 | async-start | bytes 12582912 | tf_op jit(solution)/shard_map/all_to_all | solution.py:103

commit v7 on v6

--- a/solution.py
+++ b/solution.py
@@ -85,10 +85,9 @@
             == jnp.bitwise_xor(occ_js[:, None], a_lab[None, :])[None]
         )
         i_blk = jnp.where(sym, i_blk, zero_bf)
-        blk = lax.dot_general(
-            jnp.transpose(i_blk, (2, 1, 0)), a_blk, (((2,), (2,)), ((), ())),
-            preferred_element_type=jnp.float32,
-        )
+        lhs = jnp.transpose(i_blk, (2, 1, 0)).reshape(width * j_slab, width)
+        rhs = a_blk.reshape(i_slab * width, width)
+        blk = lax.dot_general(lhs, rhs, (((1,), (1,)), ((), ())), preferred_element_type=jnp.float32)
         per_g.append(blk.reshape(width, -1))
     every = jnp.concatenate(per_g, axis=0)
     b_pos = jnp.arange(v_width, dtype=jnp.int32)

time: 241 us -> 266 us (1.10)
  local copies, waits for them, and re-layouts: 49.5 us -> 62.1 us
  other arithmetic: 19 us -> 28.7 us
    select_n x0 -> x2, other arithmetic: none -> 8.95 us  [body(): a_blk = jnp.where(allowed, a_blk, zero_bf)]
    transpose x0 -> x8, local copies, waits for them, and re-layouts: none -> 8.03 us  [body(): lhs = jnp.transpose(i_blk, (2, 1, 0)).reshape(width * j_slab, width)]
    reshape x0 -> x8, local copies, waits for them, and re-layouts: none -> 6.31 us  [body(): lhs = jnp.transpose(i_blk, (2, 1, 0)).reshape(width * j_slab, width)]
    unnamed x19 -> x29, local copies, waits for them, and re-layouts: 14.4 us -> 9.23 us
    reshape x8, local copies, waits for them, and re-layouts: 11.9 us -> 15.4 us  [body(): per_g.append(blk.reshape(width, -1))]
    transpose x0 -> x2, other arithmetic: none -> 2.68 us  [body(): lhs = jnp.transpose(i_blk, (2, 1, 0)).reshape(width * j_slab, width)]
  transfers between devices with their start and end apart: 2 -> 2, of which waited for: 1 -> 1; matrix products, arithmetic and copies ran while one was open for 5% -> 7% of each run, Pallas kernels for 0% -> 0%
where the time goes in v7:
time: 266 us; the launch traced here: 264 us
  waiting for transfers between devices  78.8 us (30%)
  local copies, waits for them, and re-layouts  62.1 us (23%)
  between operations  39.3 us (15%)
  other arithmetic  28.7 us (11%)
  matrix products  25.1 us (9%)
  starting transfers between devices  18.3 us (7%)
  blocking collectives  12.1 us (5%)
    all_to_all x1, waiting for transfers between devices, body(): lax.all_to_all(compact.reshape(n_all, nb_all, -1), ('redist', 'rep'), 0,...  78.8 us
    reshape x8, local copies, waits for them, and re-layouts, body(): per_g.append(blk.reshape(width, -1))  15.4 us
    dot_general x8, matrix products, body(): lax.dot_general(lhs, rhs, (((1,), (1,)), ((), ())), preferred_element_typ...  15.1 us
    all_gather x1, blocking collectives, body(): mine_b = lax.all_gather(summed, 'rep', axis=0, tiled=True)  12.1 us
    gather x1, local copies, waits for them, and re-layouts, body(): compact = jnp.take(every, pick, axis=0, mode='clip')  11.4 us
    all_to_all x1, starting transfers between devices, body(): lax.all_to_all(compact.reshape(n_all, nb_all, -1), ('redist', 'rep'), 0,...  10.6 us
    dot_general x1, matrix products, body(): lax.dot_general(ints_mine, selector, (((3,), (1,)), ((), ())), preferred_...  10 us
    unnamed x29, local copies, waits for them, and re-layouts  9.23 us
  transfers between devices with their start and end apart: 2, of which 1 were waited for; matrix products, arithmetic and copies ran while one was open for 7% of the time, Pallas kernels for 0%

profile of v7, /device:TPU:6, one launch (start us, length us, event | category | flops | bytes accessed | tf_op | source)
XLA Modules:
  0.0 264.3 jit_solution(14642775932436572706)
XLA Ops:
  0.0 0.8 convert_reduce_fusion
  0.8 0.8 dynamic_slice.148
  1.7 0.7 reshape.846
  2.4 5.6 %constant_dynamic-slice_fusion = bf16[32,1,1,32,2,1024]{5,4,3,1,0,2:T(2,128)(2,1)S(1)} fusion(bf16[32,4,1,32,2,1024]{5,4,3,1,0,2:T(2,128)(2,1)} %bitcast.152, s32[]{:T(128)S(6)} %select_n.258), kind=kLoop, calls=%fused_computation.76 | loop fusion | bytes 8388612 | tf_op jit(solution)/shard_map/dynamic_slice | solution.py:47
  8.2 10.0 %fusion.1 = bf16[32,32,2,8,192]{4,1,3,2,0:T(8,128)(2,1)S(1)} fusion(bf16[32,1,1,32,2,1024]{5,4,3,1,0,2:T(2,128)(2,1)S(1)} %constant_dynamic-slice_fusion, s32[8,192]{1,0:T(8,128)S(1)} %iota_add_fusion), kind=kOutput, calls=%fused_computation.3 | convolution fusion | flops 6444023808 | bytes 10491904 | tf_op jit(solution)/shard_map/dot_general | solution.py:60
  18.3 2.4 fusion.11
  20.7 7.6 %all-to-all-start = ((bf16[32,32,2,192]{3,1,2,0:T(8,128)(2,1)}), bf16[32,32,2,192]{3,1,2,0:T(8,128)(2,1)S(1)}, u32[]{:S(2)}, u32[]{:S(2)}) async-start(bf16[32,32,2,192]{3,1,2,0:T(8,128)(2,1)} %fusion.11), calls=%async_computation | async-start | bytes 2097152 | tf_op jit(solution)/shard_map/all_to_all | solution.py:67
  28.4 0.7 dynamic_slice.149
  35.3 0.7 fusion.22
  56.2 4.9 %add_clamp_fusion = s32[1024]{0:T(1024)S(1)} fusion(s32[1024]{0:T(1024)S(1)} %copy-done.9, s32[]{:T(128)} %bitcast.3, s32[]{:T(128)} %bitcast.22, s32[]{:T(128)} %bitcast.26, s32[]{:T(128)} %bitcast.30, s32[]{:T(128)} %bitcast.34, s32[]{:T(128)} %bitcast.38, s32[]{:T(128)} %bitcast.42, s32[]{:T(128)} %bitcast.46), kind=kLoop, calls=%fused_computation.77 | loop fusion | flops 20480 | bytes 8224 | tf_op jit(solution)/shard_map/jit(_take)/gather | solution.py:98
  71.2 0.7 broadcast_compare_fusion
  72.0 0.6 broadcast_xor_fusion.20
  72.6 0.6 broadcast_xor_fusion.22
  73.2 0.6 broadcast_xor_fusion.16
  74.2 0.6 broadcast_xor_fusion.18
  75.2 0.6 slice_xor_fusion
  75.8 3.5 %compare_select_fusion.1 = (bf16[4,1,192,192]{3,2,1,0:T(8,128)(2,1)}, bf16[4,1,192,192]{3,2,1,0:T(8,128)(2,1)}, bf16[4,1,192,192]{3,2,1,0:T(8,128)(2,1)S(1)}) fusion(bf16[4,1,1024,1024]{3,2,1,0:T(8,128)(2,1)} %param.4, s32[]{:T(128)S(6)} %select_n.301, s32[]{:T(128)S(6)} %select_n.300, s32[192,192]{1,0:T(8,128)S(1)} %get-tuple-element.101, ...), kind=kLoop, calls=%fused_computation.26 | loop fusion | flops 884736 | bytes 2211880 | tf_op jit(solution)/shard_map/jit(_where)/select_n | solution.py:81
  79.3 5.4 %compare_select_fusion = (bf16[4,1,192,192]{3,2,1,0:T(8,128)(2,1)}, bf16[4,1,192,192]{3,2,1,0:T(8,128)(2,1)}, bf16[4,1,192,192]{3,2,1,0:T(8,128)(2,1)}, bf16[4,1...) fusion(bf16[4,1,1024,1024]{3,2,1,0:T(8,128)(2,1)} %param.4, s32[]{:T(128)S(6)} %select_n.307, s32[]{:T(128)S(6)} %select_n.306, ...), kind=kLoop, calls=%fused_computation.25 | loop fusion | flops 1474560 | bytes 3686456 | tf_op jit(solution)/shard_map/jit(_where)/select_n | solution.py:81
  84.8 1.3 fusion.16
  86.3 0.2 reshape.849
  86.5 0.4 fusion.23
  86.9 0.3 reshape.850
  87.2 1.1 constant_dynamic-update-slice_fusion.7
  88.3 1.1 copy.41
  89.4 0.2 reshape.851
  89.6 1.4 fusion.24
  91.0 0.3 reshape.852
  91.3 1.1 copy.42
  92.4 0.2 reshape.853
  92.6 2.4 fusion.25
  95.0 1.6 reshape.854
  96.6 1.8 copy.43
  98.4 1.8 reshape.855
  100.2 2.5 fusion.26
  102.7 2.6 reshape.856
  105.3 1.4 fusion.20
  106.7 1.2 copy.44
  108.0 2.4 fusion.27
  110.4 2.6 reshape.858
  113.1 0.8 copy.45
  113.9 1.8 reshape.859
  115.7 2.3 fusion.28
  118.0 2.7 %reshape.860 = f32[192,1536]{1,0:T(8,128)} reshape(f32[384,768]{1,0:T(8,128)} %fusion.28) | data formatting | bytes 2359296 | tf_op jit(solution)/shard_map/reshape | solution.py:91
  120.7 1.8 copy.46
  122.5 1.8 reshape.861
  124.3 2.3 fusion.29
  126.6 2.6 reshape.862
  129.6 1.4 fusion.30
  130.9 2.6 reshape.864
  133.5 1.1 constant_dynamic-update-slice_fusion.6
  134.6 1.1 constant_dynamic-update-slice_fusion.5
  135.8 2.5 constant_dynamic-update-slice_fusion.4
  138.2 1.1 constant_dynamic-update-slice_fusion.3
  139.4 1.1 constant_dynamic-update-slice_fusion.2
  140.5 1.1 constant_dynamic-update-slice_fusion.1
  141.6 1.2 constant_dynamic-update-slice_fusion
  142.8 11.4 %gather_fusion = f32[1024,1536]{1,0:T(8,128)} fusion(f32[1536,1536]{1,0:T(8,128)} %constant_dynamic-update-slice_fusion, s32[1024]{0:T(1024)S(1)} %add_clamp_fusion), kind=kCustom, calls=%fused_computation | custom fusion | bytes 12587008 | tf_op jit(solution)/shard_map/jit(_take)/gather | solution.py:98
  154.2 10.6 %all-to-all-start.1 = ((f32[128,8,1536]{2,1,0:T(8,128)}), f32[128,8,1536]{2,1,0:T(8,128)}, u32[]{:S(2)}, u32[]{:S(2)}) async-start(f32[128,8,1536]{2,1,0:T(8,128)} %bitcast.141), calls=%async_computation.1 | async-start | bytes 12582912 | tf_op jit(solution)/shard_map/all_to_all | solution.py:102
  167.3 78.8 %all-to-all-done.1 = f32[128,8,1536]{2,1,0:T(8,128)} async-done(((f32[128,8,1536]{2,1,0:T(8,128)}), f32[128,8,1536]{2,1,0:T(8,128)}, u32[]{:S(2)}, u32[]{:S(2)}) %all-to-all-start.1) | async-done | bytes 6291488 | tf_op jit(solution)/shard_map/all_to_all | solution.py:102
  246.1 3.1 %reduce_sum.19 = f32[8,1536]{1,0:T(8,128)S(1)} reduce(f32[128,8,1536]{2,1,0:T(8,128)} %all-to-all-done.1, f32[]{:T(128)} %constant.78.clone.1), dimensions={0}, to_apply=%region_1.2 | reduce | flops 1560576 | bytes 6340612 | tf_op jit(solution)/shard_map/reduce_sum | solution.py:103
  249.2 12.1 %all_gather.3 = f32[32,1536]{1,0:T(8,128)S(1)} all-gather(f32[8,1536]{1,0:T(8,128)S(1)} %reduce_sum.19), channel_id=1, replica_groups=mesh['redist'=32,'rep'=4] {'rep'}, dimensions={0}, use_global_device_ids=true | all-gather | bytes 245760 | tf_op jit(solution)/shard_map/all_gather | solution.py:104
  261.3 0.2 reshape.866
  261.6 1.2 fusion.12
  262.7 1.6 copy.48
  (39 shorter events, 1.9 us)
Async XLA Ops:
  18.3 10.1 %copy-start.10 = (s32[128]{0:T(128)S(1)}, s32[128]{0:T(128)}, u32[]{:S(2)}) copy-start(s32[128]{0:T(128)} %param.6) | copy-start | bytes 1540
  18.3 38.0 %copy-start.9 = (s32[1024]{0:T(1024)S(1)}, s32[1024]{0:T(1024)}, u32[]{:S(2)}) copy-start(s32[1024]{0:T(1024)} %param.7) | copy-start | bytes 12292
  20.7 64.1 %all-to-all-start = ((bf16[32,32,2,192]{3,1,2,0:T(8,128)(2,1)}), bf16[32,32,2,192]{3,1,2,0:T(8,128)(2,1)S(1)}, u32[]{:S(2)}, u32[]{:S(2)}) async-start(bf16[32,32,2,192]{3,1,2,0:T(8,128)(2,1)} %fusion.11), calls=%async_computation | async-start | bytes 2097152 | tf_op jit(solution)/shard_map/all_to_all | solution.py:67
  106.7 6.4 %copy-start.8 = (bf16[192,2,192]{0,2,1:T(8,128)(2,1)S(1)}, bf16[192,2,192]{0,2,1:T(8,128)(2,1)}, u32[]{:S(2)}) copy-start(bf16[192,2,192]{0,2,1:T(8,128)(2,1)} %get-tuple-element.31) | copy-start | bytes 442372
  106.7 9.0 %copy-start.5 = (bf16[4,1,192,192]{3,2,1,0:T(8,128)(2,1)S(1)}, bf16[4,1,192,192]{3,2,1,0:T(8,128)(2,1)}, u32[]{:S(2)}) copy-start(bf16[4,1,192,192]{3,2,1,0:T(8,128)(2,1)} %get-tuple-element.22) | copy-start | bytes 884740
  110.4 13.9 %copy-start.6 = (bf16[4,1,192,192]{3,2,1,0:T(8,128)(2,1)S(1)}, bf16[4,1,192,192]{3,2,1,0:T(8,128)(2,1)}, u32[]{:S(2)}) copy-start(bf16[4,1,192,192]{3,2,1,0:T(8,128)(2,1)} %get-tuple-element.26) | copy-start | bytes 884740
  115.7 13.5 %copy-start.7 = (bf16[192,2,192]{0,2,1:T(8,128)(2,1)S(1)}, bf16[192,2,192]{0,2,1:T(8,128)(2,1)}, u32[]{:S(2)}) copy-start(bf16[192,2,192]{0,2,1:T(8,128)(2,1)} %get-tuple-element.29) | copy-start | bytes 442372
  118.0 11.5 %copy-start.4 = (bf16[4,1,192,192]{3,2,1,0:T(8,128)(2,1)S(1)}, bf16[4,1,192,192]{3,2,1,0:T(8,128)(2,1)}, u32[]{:S(2)}) copy-start(bf16[4,1,192,192]{3,2,1,0:T(8,128)(2,1)} %get-tuple-element.21) | copy-start | bytes 884740
  133.5 4.7 %copy-start = (f32[192,1536]{1,0:T(8,128)S(1)}, f32[192,1536]{1,0:T(8,128)}, u32[]{:S(2)}) copy-start(f32[192,1536]{1,0:T(8,128)} %reshape.858) | copy-start | bytes 3538948
  133.5 5.8 %copy-start.1 = (f32[192,1536]{1,0:T(8,128)S(1)}, f32[192,1536]{1,0:T(8,128)}, u32[]{:S(2)}) copy-start(f32[192,1536]{1,0:T(8,128)} %reshape.860) | copy-start | bytes 3538948
  134.6 5.9 %copy-start.2 = (f32[192,1536]{1,0:T(8,128)S(1)}, f32[192,1536]{1,0:T(8,128)}, u32[]{:S(2)}) copy-start(f32[192,1536]{1,0:T(8,128)} %reshape.862) | copy-start | bytes 3538948
  135.8 5.9 %copy-start.3 = (f32[192,1536]{1,0:T(8,128)S(1)}, f32[192,1536]{1,0:T(8,128)}, u32[]{:S(2)}) copy-start(f32[192,1536]{1,0:T(8,128)} %reshape.864) | copy-start | bytes 3538948
  154.2 91.9 %all-to-all-start.1 = ((f32[128,8,1536]{2,1,0:T(8,128)}), f32[128,8,1536]{2,1,0:T(8,128)}, u32[]{:S(2)}, u32[]{:S(2)}) async-start(f32[128,8,1536]{2,1,0:T(8,128)} %bitcast.141), calls=%async_computation.1 | async-start | bytes 12582912 | tf_op jit(solution)/shard_map/all_to_all | solution.py:102

commit v8 on v7

--- a/solution.py
+++ b/solution.py
@@ -69,7 +69,8 @@
     k_lab = occ_irrep[dev_index * n_rep + rep_index]
     amp = amplitudes[:, 0]
     pair_ik = jnp.bitwise_xor(occ_rows, k_lab)
-    per_g = []
+    a_blks = []
+    i_blks = []
     for g in range(N_IRREPS):
         c_irrep = jnp.bitwise_xor(g, k_lab)
         wa = wins[g]
@@ -78,18 +79,18 @@
         cw_lab = lax.dynamic_slice_in_dim(virt_irrep, wc, width)
         a_blk = lax.dynamic_slice(amp, (0, wa, wc), (i_slab, width, width))
         allowed = pair_ik[:, None, None] == jnp.bitwise_xor(a_lab[:, None], cw_lab[None, :])[None]
-        a_blk = jnp.where(allowed, a_blk, zero_bf)
+        a_blks.append(jnp.where(allowed, a_blk, zero_bf))
         i_blk = lax.dynamic_slice(moved, (wc, 0, 0), (width, j_slab, width))
         sym = (cw_lab == c_irrep)[:, None, None] & (
             jnp.bitwise_xor(cw_lab, k_lab)[:, None, None]
             == jnp.bitwise_xor(occ_js[:, None], a_lab[None, :])[None]
         )
-        i_blk = jnp.where(sym, i_blk, zero_bf)
-        lhs = jnp.transpose(i_blk, (2, 1, 0)).reshape(width * j_slab, width)
-        rhs = a_blk.reshape(i_slab * width, width)
-        blk = lax.dot_general(lhs, rhs, (((1,), (1,)), ((), ())), preferred_element_type=jnp.float32)
-        per_g.append(blk.reshape(width, -1))
-    every = jnp.concatenate(per_g, axis=0)
+        i_blks.append(jnp.where(sym, i_blk, zero_bf))
+    blk = lax.dot_general(
+        jnp.transpose(jnp.stack(i_blks), (0, 3, 2, 1)), jnp.stack(a_blks),
+        (((3,), (3,)), ((0,), (0,))), preferred_element_type=jnp.float32,
+    )
+    every = blk.reshape(N_IRREPS * width, -1)
     b_pos = jnp.arange(v_width, dtype=jnp.int32)
     b_win_start = jnp.zeros_like(virt_irrep)
     for g in range(N_IRREPS):

time: 266 us -> 271 us (1.019)
  matrix products: 25.1 us -> 11.8 us
  other arithmetic: 28.7 us -> 40.2 us
  local copies, waits for them, and re-layouts: 62.1 us -> 68.2 us
    unnamed x0 -> x14, other arithmetic: none -> 17.1 us
    dot_general x8 -> x1, matrix products: 15.1 us -> 1.82 us  [body(): lax.dot_general(jnp.transpose(jnp.stack(i_blks), (0, 3, 2, 1)), jnp.stack...]
    reshape x16 -> x2, local copies, waits for them, and re-layouts: 21.7 us -> 31.5 us  [body(): every = blk.reshape(N_IRREPS * width, -1)]
    select_n x2 -> x0, other arithmetic: 8.95 us -> none  [body(): a_blk = jnp.where(allowed, a_blk, zero_bf)]
    transpose x8 -> x0, local copies, waits for them, and re-layouts: 8.03 us -> none  [body(): lhs = jnp.transpose(i_blk, (2, 1, 0)).reshape(width * j_slab, width)]
    unnamed x29 -> x14, local copies, waits for them, and re-layouts: 9.23 us -> 12.1 us
  transfers between devices with their start and end apart: 2 -> 2, of which waited for: 1 -> 1; matrix products, arithmetic and copies ran while one was open for 7% -> 10% of each run, Pallas kernels for 0% -> 0%
where the time goes in v8:
time: 271 us; the launch traced here: 269 us
  waiting for transfers between devices  78.6 us (29%)
  local copies, waits for them, and re-layouts  68.2 us (25%)
  other arithmetic  40.2 us (15%)
  between operations  39.8 us (15%)
  starting transfers between devices  18.3 us (7%)
  blocking collectives  12.1 us (4%)
  matrix products  11.8 us (4%)
    all_to_all x1, waiting for transfers between devices, body(): lax.all_to_all(compact.reshape(n_all, nb_all, -1), ('redist', 'rep'), 0,...  78.6 us
    reshape x2, local copies, waits for them, and re-layouts, body(): every = blk.reshape(N_IRREPS * width, -1)  31.5 us
    unnamed x14, other arithmetic  17.1 us
    all_gather x1, blocking collectives, body(): mine_b = lax.all_gather(summed, 'rep', axis=0, tiled=True)  12.1 us
    unnamed x14, local copies, waits for them, and re-layouts  12.1 us
    gather x1, local copies, waits for them, and re-layouts, body(): compact = jnp.take(every, pick, axis=0, mode='clip')  11.4 us
    all_to_all x1, starting transfers between devices, body(): lax.all_to_all(compact.reshape(n_all, nb_all, -1), ('redist', 'rep'), 0,...  10.6 us
    dot_general x1, matrix products, body(): lax.dot_general(ints_mine, selector, (((3,), (1,)), ((), ())), preferred_...  10 us
  transfers between devices with their start and end apart: 2, of which 1 were waited for; matrix products, arithmetic and copies ran while one was open for 10% of the time, Pallas kernels for 0%

profile of v8, /device:TPU:6, one launch (start us, length us, event | category | flops | bytes accessed | tf_op | source)
XLA Modules:
  0.0 269.1 jit_solution(3880536501174271875)
XLA Ops:
  0.0 0.8 convert_reduce_fusion
  0.8 0.8 dynamic_slice.164
  1.6 0.1 iota_add_fusion
  1.6 0.7 reshape.793
  2.4 0.2 dynamic-slice_reduce_fusion
  2.6 5.6 %constant_dynamic-slice_fusion.8 = bf16[32,1,1,32,2,1024]{5,4,3,1,0,2:T(2,128)(2,1)S(1)} fusion(bf16[32,4,1,32,2,1024]{5,4,3,1,0,2:T(2,128)(2,1)} %bitcast.163, s32[]{:T(128)S(6)} %select_n.282), kind=kLoop, calls=%fused_computation.95 | loop fusion | bytes 8388612 | tf_op jit(solution)/shard_map/dynamic_slice | solution.py:47
  8.2 0.1 xor_compare_fusion.6
  8.3 10.0 %fusion.1 = bf16[32,32,2,8,192]{4,1,3,2,0:T(8,128)(2,1)S(1)} fusion(bf16[32,1,1,32,2,1024]{5,4,3,1,0,2:T(2,128)(2,1)S(1)} %constant_dynamic-slice_fusion.8, s32[8,192]{1,0:T(8,128)S(1)} %iota_add_fusion), kind=kOutput, calls=%fused_computation.3 | convolution fusion | flops 6444023808 | bytes 10491904 | tf_op jit(solution)/shard_map/dot_general | solution.py:60
  18.3 0.0 copy-start.2
  18.3 2.4 fusion.13
  20.7 7.7 %all-to-all-start = ((bf16[32,32,2,192]{3,1,2,0:T(8,128)(2,1)}), bf16[32,32,2,192]{3,1,2,0:T(8,128)(2,1)}, u32[]{:S(2)}, u32[]{:S(2)}) async-start(bf16[32,32,2,192]{3,1,2,0:T(8,128)(2,1)} %fusion.13), calls=%async_computation | async-start | bytes 2097152 | tf_op jit(solution)/shard_map/all_to_all | solution.py:67
  28.3 0.7 dynamic_slice.165
  35.2 0.7 slice_xor_fusion
  36.7 0.7 fusion.41
  57.5 4.9 %add_clamp_fusion = s32[1024]{0:T(1024)S(1)} fusion(s32[1024]{0:T(1024)S(1)} %copy-done.1, s32[]{:T(128)} %bitcast.3, s32[]{:T(128)} %bitcast.21, s32[]{:T(128)} %bitcast.24, s32[]{:T(128)} %bitcast.27, s32[]{:T(128)} %bitcast.30, s32[]{:T(128)} %bitcast.33, s32[]{:T(128)} %bitcast.36, s32[]{:T(128)} %bitcast.39), kind=kLoop, calls=%fused_computation.96 | loop fusion | flops 20480 | bytes 8224 | tf_op jit(solution)/shard_map/jit(_take)/gather | solution.py:99
  72.4 1.4 broadcast_compare_fusion
  73.8 1.3 broadcast_xor_fusion.16
  75.1 1.3 broadcast_xor_fusion.18
  76.4 1.3 broadcast_xor_fusion.20
  77.7 0.1 fusion.40
  77.8 0.1 broadcast_xor_fusion.2
  77.9 0.1 broadcast_xor_fusion.4
  78.0 0.1 broadcast_xor_fusion
  78.1 0.7 broadcast_xor_fusion.8
  78.8 0.1 broadcast_xor_fusion.6
  78.9 1.4 fusion.16
  80.3 1.3 fusion.17
  81.6 1.4 fusion.18
  83.0 1.4 fusion.19
  84.3 1.4 fusion.20
  85.7 1.3 broadcast_xor_fusion.22
  87.0 1.3 fusion.21
  88.3 1.4 fusion.22
  89.7 1.4 fusion.23
  91.1 1.3 copy.41
  92.4 1.4 constant_dynamic-slice_fusion
  93.8 1.7 copy.74
  95.5 1.7 copy.73
  97.3 1.7 copy.72
  99.0 1.7 copy.71
  100.7 1.7 copy.70
  102.5 1.7 copy.69
  104.2 0.8 copy.68
  105.1 0.8 copy.67
  105.9 1.1 fusion.25
  107.0 1.1 fusion.27
  108.1 1.1 fusion.29
  109.2 1.1 fusion.31
  110.2 1.1 fusion.33
  111.3 1.1 fusion.35
  112.4 1.1 fusion.37
  113.5 0.8 fusion.39
  114.4 1.8 fusion.3
  116.2 16.7 %copy.57 = f32[8,192,2,4,192]{4,3,2,1,0:T(4,128)} copy(f32[8,192,2,4,192]{4,1,3,2,0:T(8,128)S(1)} %fusion.3) | data formatting | bytes 18874368 | tf_op jit(solution)/shard_map/reshape | solution.py:93
  132.9 14.7 %reshape.812 = f32[1536,1536]{1,0:T(8,128)} reshape(f32[8,192,2,4,192]{4,3,2,1,0:T(4,128)} %copy.57) | data formatting | bytes 18874368 | tf_op jit(solution)/shard_map/reshape | solution.py:93
  147.7 11.4 %gather_fusion = f32[1024,1536]{1,0:T(8,128)} fusion(f32[1536,1536]{1,0:T(8,128)} %reshape.812, s32[1024]{0:T(1024)S(1)} %add_clamp_fusion), kind=kCustom, calls=%fused_computation | custom fusion | bytes 12587008 | tf_op jit(solution)/shard_map/jit(_take)/gather | solution.py:99
  159.0 10.6 %all-to-all-start.1 = ((f32[128,8,1536]{2,1,0:T(8,128)}), f32[128,8,1536]{2,1,0:T(8,128)}, u32[]{:S(2)}, u32[]{:S(2)}) async-start(f32[128,8,1536]{2,1,0:T(8,128)} %bitcast.161), calls=%async_computation.1 | async-start | bytes 12582912 | tf_op jit(solution)/shard_map/all_to_all | solution.py:103
  172.2 0.1 broadcast_compare_fusion.8
  172.3 78.6 %all-to-all-done.1 = f32[128,8,1536]{2,1,0:T(8,128)} async-done(((f32[128,8,1536]{2,1,0:T(8,128)}), f32[128,8,1536]{2,1,0:T(8,128)}, u32[]{:S(2)}, u32[]{:S(2)}) %all-to-all-start.1) | async-done | bytes 6291488 | tf_op jit(solution)/shard_map/all_to_all | solution.py:103
  250.9 3.1 %reduce_sum.19 = f32[8,1536]{1,0:T(8,128)S(1)} reduce(f32[128,8,1536]{2,1,0:T(8,128)} %all-to-all-done.1, f32[]{:T(128)} %constant.78.clone.1), dimensions={0}, to_apply=%region_1.2 | reduce | flops 1560576 | bytes 6340612 | tf_op jit(solution)/shard_map/reduce_sum | solution.py:104
  254.0 12.1 %all_gather.3 = f32[32,1536]{1,0:T(8,128)S(1)} all-gather(f32[8,1536]{1,0:T(8,128)S(1)} %reduce_sum.19), channel_id=1, replica_groups=mesh['redist'=32,'rep'=4] {'rep'}, dimensions={0}, use_global_device_ids=true | all-gather | bytes 245760 | tf_op jit(solution)/shard_map/all_gather | solution.py:105
  266.1 0.2 reshape.798
  266.4 1.2 fusion.15
  267.6 1.6 copy.52
  (7 shorter events, 0.0 us)
Async XLA Ops:
  18.3 10.1 %copy-start.2 = (s32[128]{0:T(128)S(1)}, s32[128]{0:T(128)}, u32[]{:S(2)}) copy-start(s32[128]{0:T(128)} %param.6) | copy-start | bytes 1540
  18.3 39.2 %copy-start.1 = (s32[1024]{0:T(1024)S(1)}, s32[1024]{0:T(1024)}, u32[]{:S(2)}) copy-start(s32[1024]{0:T(1024)} %param.7) | copy-start | bytes 12292
  20.7 70.4 %all-to-all-start = ((bf16[32,32,2,192]{3,1,2,0:T(8,128)(2,1)}), bf16[32,32,2,192]{3,1,2,0:T(8,128)(2,1)}, u32[]{:S(2)}, u32[]{:S(2)}) async-start(bf16[32,32,2,192]{3,1,2,0:T(8,128)(2,1)} %fusion.13), calls=%async_computation | async-start | bytes 2097152 | tf_op jit(solution)/shard_map/all_to_all | solution.py:67
  105.1 8.5 %copy-start = (bf16[192,2,192]{0,2,1:T(8,128)(2,1)S(1)}, bf16[192,2,192]{0,2,1:T(8,128)(2,1)}, u32[]{:S(2)}) copy-start(bf16[192,2,192]{0,2,1:T(8,128)(2,1)} %copy.74) | copy-start | bytes 442372
  159.0 91.9 %all-to-all-start.1 = ((f32[128,8,1536]{2,1,0:T(8,128)}), f32[128,8,1536]{2,1,0:T(8,128)}, u32[]{:S(2)}, u32[]{:S(2)}) async-start(f32[128,8,1536]{2,1,0:T(8,128)} %bitcast.161), calls=%async_computation.1 | async-start | bytes 12582912 | tf_op jit(solution)/shard_map/all_to_all | solution.py:103

commit v9 on v6

--- a/solution.py
+++ b/solution.py
@@ -102,7 +102,12 @@
     nb_all = v_width // n_all
     pieces = lax.all_to_all(compact.reshape(n_all, nb_all, -1), ("redist", "rep"), 0, 0, tiled=True)
     summed = jnp.sum(pieces, axis=0)
-    mine_b = lax.all_gather(summed, "rep", axis=0, tiled=True)
+    got = [summed] + [
+        lax.ppermute(summed, "rep", [(z, (z + s) % n_rep) for z in range(n_rep)])
+        for s in range(1, n_rep)
+    ]
+    order = (rep_index - jnp.arange(n_rep, dtype=jnp.int32)) % n_rep
+    mine_b = jnp.take(jnp.stack(got), order, axis=0, mode="clip").reshape(n_rep * nb_all, -1)
 
     nb = mine_b.shape[0]
     vals = mine_b.reshape(nb, j_slab, i_slab, width).transpose(2, 3, 1, 0)

time: 241 us -> 237 us (0.983)
  blocking collectives: 12.1 us -> 0 us
  waiting for transfers between devices: 78.6 us -> 82.4 us
  starting transfers between devices: 18.3 us -> 21.6 us
    all_gather x1 -> x0, blocking collectives: 12.1 us -> none  [body(): mine_b = lax.all_gather(summed, 'rep', axis=0, tiled=True)]
    ppermute x0 -> x3, starting transfers between devices: none -> 3.29 us  [body(): lax.ppermute(summed, 'rep', [(z, (z + s) % n_rep) for z in range(n_rep)])]
    all_to_all x1, waiting for transfers between devices: 78.6 us -> 81.2 us  [body(): lax.all_to_all(compact.reshape(n_all, nb_all, -1), ('redist', 'rep'), 0,...]
  transfers between devices with their start and end apart: 2 -> 5, of which waited for: 1 -> 3; matrix products, arithmetic and copies ran while one was open for 5% -> 6% of each run, Pallas kernels for 0% -> 0%
where the time goes in v9:
time: 237 us; the launch traced here: 236 us
  waiting for transfers between devices  82.4 us (35%)
  local copies, waits for them, and re-layouts  50 us (21%)
  between operations  39.7 us (17%)
  matrix products  23 us (10%)
  starting transfers between devices  21.6 us (9%)
  other arithmetic  19.3 us (8%)
    all_to_all x1, waiting for transfers between devices, body(): lax.all_to_all(compact.reshape(n_all, nb_all, -1), ('redist', 'rep'), 0,...  81.2 us
    unnamed x19, local copies, waits for them, and re-layouts  14.4 us
    dot_general x8, matrix products, body(): lax.dot_general(jnp.transpose(i_blk, (2, 1, 0)), a_blk, (((2,), (2,)), ((...  13 us
    reshape x8, local copies, waits for them, and re-layouts, body(): per_g.append(blk.reshape(width, -1))  11.9 us
    gather x1, local copies, waits for them, and re-layouts, body(): compact = jnp.take(every, pick, axis=0, mode='clip')  11.4 us
    all_to_all x1, starting transfers between devices, body(): lax.all_to_all(compact.reshape(n_all, nb_all, -1), ('redist', 'rep'), 0,...  10.7 us
    dot_general x1, matrix products, body(): lax.dot_general(ints_mine, selector, (((3,), (1,)), ((), ())), preferred_...  10 us
    all_to_all x1, starting transfers between devices, body(): lax.all_to_all(packed, 'redist', split_axis=0, concat_axis=1, tiled=True)[0]  7.61 us
  transfers between devices with their start and end apart: 5, of which 3 were waited for; matrix products, arithmetic and copies ran while one was open for 6% of the time, Pallas kernels for 0%

profile of v9, /device:TPU:6, one launch (start us, length us, event | category | flops | bytes accessed | tf_op | source)
XLA Modules:
  0.0 235.9 jit_solution(10056588059466403291)
XLA Ops:
  0.0 0.8 convert_reduce_fusion
  0.8 0.8 dynamic_slice.164
  1.6 0.7 reshape.747
  2.3 0.2 dynamic-slice_reduce_fusion
  2.5 5.6 %constant_dynamic-slice_fusion = bf16[32,1,1,32,2,1024]{5,4,3,1,0,2:T(2,128)(2,1)S(1)} fusion(bf16[32,4,1,32,2,1024]{5,4,3,1,0,2:T(2,128)(2,1)} %bitcast.252, s32[]{:T(128)S(6)} %select_n.240), kind=kLoop, calls=%fused_computation.181 | loop fusion | bytes 8388612 | tf_op jit(solution)/shard_map/dynamic_slice | solution.py:47
  8.1 0.1 iota_add_fusion
  8.2 0.1 xor_compare_fusion.6
  8.2 10.0 %fusion.1 = bf16[32,32,2,8,192]{4,1,3,2,0:T(8,128)(2,1)S(1)} fusion(bf16[32,1,1,32,2,1024]{5,4,3,1,0,2:T(2,128)(2,1)S(1)} %constant_dynamic-slice_fusion, s32[8,192]{1,0:T(8,128)S(1)} %iota_add_fusion), kind=kOutput, calls=%fused_computation.4 | convolution fusion | flops 6444023808 | bytes 10491904 | tf_op jit(solution)/shard_map/dot_general | solution.py:60
  18.3 2.4 %fusion.11 = bf16[32,32,2,192]{3,1,2,0:T(8,128)(2,1)} fusion(bf16[32,32,2,8,192]{4,1,3,2,0:T(8,128)(2,1)S(1)} %fusion.1, pred[32,32]{1,0:T(8,128)(4,1)S(1)} %get-tuple-element.44, pred[32,32]{1,0:T(8,128)(4,1)S(1)} %get-tuple-element.45, pred[32,32]{1,0:T(8,128)(4,1)S(1)} %get-tuple-element.46, pred[32,32]{1,0:T(8,128)(4,1)S(1)} %get-tuple-element.47, ...), kind=kLoop, calls=%fused_computation.17 | loop fusion | flops 2752512 | bytes 7085056 | tf_op jit(solution)/shard_map/convert_element_type | solution.py:66
  20.6 7.6 %all-to-all-start = ((bf16[32,32,2,192]{3,1,2,0:T(8,128)(2,1)}), bf16[32,32,2,192]{3,1,2,0:T(8,128)(2,1)S(1)}, u32[]{:S(2)}, u32[]{:S(2)}) async-start(bf16[32,32,2,192]{3,1,2,0:T(8,128)(2,1)} %fusion.11), calls=%async_computation | async-start | bytes 2097152 | tf_op jit(solution)/shard_map/all_to_all | solution.py:67
  28.3 0.6 dynamic_slice.165
  35.4 0.7 fusion.152
  56.3 5.0 %add_clamp_fusion = s32[1024]{0:T(1024)S(1)} fusion(s32[1024]{0:T(1024)S(1)} %copy-done.4, s32[]{:T(128)} %bitcast.3, s32[]{:T(128)} %bitcast.25, s32[]{:T(128)} %bitcast.32, s32[]{:T(128)} %bitcast.39, s32[]{:T(128)} %bitcast.46, s32[]{:T(128)} %bitcast.53, s32[]{:T(128)} %bitcast.60, s32[]{:T(128)} %bitcast.67), kind=kLoop, calls=%fused_computation.184 | loop fusion | flops 20480 | bytes 8224 | tf_op jit(solution)/shard_map/jit(_take)/gather | solution.py:99
  71.5 0.7 broadcast_compare_fusion
  72.2 0.6 broadcast_xor_fusion.22
  72.8 0.1 fusion.151
  72.9 0.8 broadcast_xor_fusion.6
  73.7 0.6 broadcast_xor_fusion.20
  74.4 0.6 broadcast_xor_fusion.18
  75.0 0.6 broadcast_xor_fusion.16
  75.6 0.1 broadcast_xor_fusion.8
  75.7 0.6 slice_xor_fusion
  76.4 0.9 broadcast_xor_fusion.4
  77.3 0.8 broadcast_xor_fusion.2
  78.0 0.1 broadcast_xor_fusion
  78.2 0.1 copy.55
  78.3 1.6 fusion.14
  79.9 1.5 copy.64
  81.4 2.4 %constant_dynamic-update-slice_fusion.7 = f32[1536,1536]{1,0:T(8,128)} fusion(f32[192,1536]{1,0:T(8,128)} %copy.64), kind=kLoop, calls=%fused_computation.171 | loop fusion | bytes 2359296
  83.7 1.5 fusion.17
  85.3 1.5 copy.65
  86.8 1.7 fusion.20
  88.5 1.5 copy.66
  90.0 1.7 fusion.23
  91.6 1.5 copy.67
  93.1 1.6 fusion.26
  94.7 1.5 copy.68
  96.2 1.6 fusion.29
  97.8 1.5 copy.69
  99.3 1.6 fusion.32
  101.0 1.5 copy.70
  102.4 1.6 fusion.35
  104.1 1.5 copy.71
  105.6 2.5 %constant_dynamic-update-slice_fusion.6 = f32[1536,1536]{1,0:T(8,128)} fusion(f32[1536,1536]{1,0:T(8,128)} %constant_dynamic-update-slice_fusion.7, f32[192,1536]{1,0:T(8,128)} %copy.65), kind=kLoop, calls=%fused_computation.170 | loop fusion | bytes 2359296
  108.1 2.5 %constant_dynamic-update-slice_fusion.5 = f32[1536,1536]{1,0:T(8,128)} fusion(f32[1536,1536]{1,0:T(8,128)} %constant_dynamic-update-slice_fusion.6, f32[192,1536]{1,0:T(8,128)} %copy.66), kind=kLoop, calls=%fused_computation.169 | loop fusion | bytes 2359296
  110.5 2.4 %constant_dynamic-update-slice_fusion.4 = f32[1536,1536]{1,0:T(8,128)} fusion(f32[1536,1536]{1,0:T(8,128)} %constant_dynamic-update-slice_fusion.5, f32[192,1536]{1,0:T(8,128)} %copy.67), kind=kLoop, calls=%fused_computation.168 | loop fusion | bytes 2359296
  112.9 1.1 constant_dynamic-update-slice_fusion.3
  114.0 2.4 %constant_dynamic-update-slice_fusion.2 = f32[1536,1536]{1,0:T(8,128)} fusion(f32[1536,1536]{1,0:T(8,128)} %constant_dynamic-update-slice_fusion.3, f32[192,1536]{1,0:T(8,128)} %copy.69), kind=kLoop, calls=%fused_computation.166 | loop fusion | bytes 2359296
  116.4 1.1 constant_dynamic-update-slice_fusion.1
  117.6 1.2 constant_dynamic-update-slice_fusion
  118.7 11.4 %gather_fusion = f32[1024,1536]{1,0:T(8,128)} fusion(f32[1536,1536]{1,0:T(8,128)} %constant_dynamic-update-slice_fusion, s32[1024]{0:T(1024)S(1)} %add_clamp_fusion), kind=kCustom, calls=%fused_computation | custom fusion | bytes 12587008 | tf_op jit(solution)/shard_map/jit(_take)/gather | solution.py:99
  130.2 10.7 %all-to-all-start.1 = ((f32[128,8,1536]{2,1,0:T(8,128)}), f32[128,8,1536]{2,1,0:T(8,128)}, u32[]{:S(2)}, u32[]{:S(2)}) async-start(f32[128,8,1536]{2,1,0:T(8,128)} %bitcast.235), calls=%async_computation.1 | async-start | bytes 12582912 | tf_op jit(solution)/shard_map/all_to_all | solution.py:103
  140.9 81.2 %all-to-all-done.1 = f32[128,8,1536]{2,1,0:T(8,128)} async-done(((f32[128,8,1536]{2,1,0:T(8,128)}), f32[128,8,1536]{2,1,0:T(8,128)}, u32[]{:S(2)}, u32[]{:S(2)}) %all-to-all-start.1) | async-done | bytes 6291488 | tf_op jit(solution)/shard_map/all_to_all | solution.py:103
  222.0 3.1 %reduce_sum.19 = f32[8,1536]{1,0:T(8,128)S(1)} reduce(f32[128,8,1536]{2,1,0:T(8,128)} %all-to-all-done.1, f32[]{:T(128)} %constant.89.clone.1), dimensions={0}, to_apply=%region_1.2 | reduce | flops 1560576 | bytes 6340612 | tf_op jit(solution)/shard_map/reduce_sum | solution.py:104
  225.2 0.1 collective-permute-start
  225.3 0.1 collective-permute-start.1
  225.3 3.1 %collective-permute-start.2 = (f32[8,1536]{1,0:T(8,128)S(1)}, f32[8,1536]{1,0:T(8,128)S(1)}, u32[]{:S(2)}, u32[]{:S(2)}) collective-permute-start(f32[8,1536]{1,0:T(8,128)S(1)} %reduce_sum.19), channel_id=1, source_target_pairs={{0,3},{1,0},{2,1},{3,2},{4,7},{5,4},{6,5},{7,6},{8,11},{9,8},{10,9... | collective-permute-start | bytes 147464 | tf_op jit(solution)/shard_map/ppermute | solution.py:106
  228.5 0.1 broadcast_compare_fusion.8
  231.2 0.2 collective-permute-done
  231.4 0.9 collective-permute-done.2
  232.3 0.6 gather_fusion.1
  232.9 0.2 reshape_reshape.3
  233.1 1.2 fusion.12
  234.3 1.6 copy.72
  (18 shorter events, 0.1 us)
Async XLA Ops:
  18.3 10.0 %copy-start.5 = (s32[128]{0:T(128)S(1)}, s32[128]{0:T(128)}, u32[]{:S(2)}) copy-start(s32[128]{0:T(128)} %param.6) | copy-start | bytes 1540
  18.3 38.1 %copy-start.4 = (s32[1024]{0:T(1024)S(1)}, s32[1024]{0:T(1024)}, u32[]{:S(2)}) copy-start(s32[1024]{0:T(1024)} %param.7) | copy-start | bytes 12292
  20.6 57.5 %all-to-all-start = ((bf16[32,32,2,192]{3,1,2,0:T(8,128)(2,1)}), bf16[32,32,2,192]{3,1,2,0:T(8,128)(2,1)S(1)}, u32[]{:S(2)}, u32[]{:S(2)}) async-start(bf16[32,32,2,192]{3,1,2,0:T(8,128)(2,1)} %fusion.11), calls=%async_computation | async-start | bytes 2097152 | tf_op jit(solution)/shard_map/all_to_all | solution.py:67
  85.3 7.8 %copy-start.3 = (s32[192,192]{1,0:T(8,128)S(1)}, s32[192,192]{1,0:T(8,128)}, u32[]{:S(2)}) copy-start(s32[192,192]{1,0:T(8,128)} %get-tuple-element.87) | copy-start | bytes 442372
  105.5 7.4 %copy-start = (f32[192,1536]{1,0:T(8,128)S(1)}, f32[192,1536]{1,0:T(8,128)}, u32[]{:S(2)}) copy-start(f32[192,1536]{1,0:T(8,128)} %copy.68) | copy-start | bytes 3538948
  105.5 10.9 %copy-start.1 = (f32[192,1536]{1,0:T(8,128)S(1)}, f32[192,1536]{1,0:T(8,128)}, u32[]{:S(2)}) copy-start(f32[192,1536]{1,0:T(8,128)} %copy.70) | copy-start | bytes 3538948
  108.1 9.5 %copy-start.2 = (f32[192,1536]{1,0:T(8,128)S(1)}, f32[192,1536]{1,0:T(8,128)}, u32[]{:S(2)}) copy-start(f32[192,1536]{1,0:T(8,128)} %copy.71) | copy-start | bytes 3538948
  130.2 91.9 %all-to-all-start.1 = ((f32[128,8,1536]{2,1,0:T(8,128)}), f32[128,8,1536]{2,1,0:T(8,128)}, u32[]{:S(2)}, u32[]{:S(2)}) async-start(f32[128,8,1536]{2,1,0:T(8,128)} %bitcast.235), calls=%async_computation.1 | async-start | bytes 12582912 | tf_op jit(solution)/shard_map/all_to_all | solution.py:103
  225.2 6.2 %collective-permute-start = (f32[8,1536]{1,0:T(8,128)S(1)}, f32[8,1536]{1,0:T(8,128)S(1)}, u32[]{:S(2)}, u32[]{:S(2)}) collective-permute-start(f32[8,1536]{1,0:T(8,128)S(1)} %reduce_sum.19), channel_id=1, source_target_pairs={{0,1},{1,2},{2,3},{3,0},{4,5},{5,6},{6,7},{7,4},{8,9},{9,10},{10,1... | collective-permute-start | bytes 147464 | tf_op jit(solution)/shard_map/ppermute | solution.py:106
  225.3 6.1 %collective-permute-start.1 = (f32[8,1536]{1,0:T(8,128)S(1)}, f32[8,1536]{1,0:T(8,128)S(1)}, u32[]{:S(2)}, u32[]{:S(2)}) collective-permute-start(f32[8,1536]{1,0:T(8,128)S(1)} %reduce_sum.19), channel_id=1, source_target_pairs={{0,2},{1,3},{2,0},{3,1},{4,6},{5,7},{6,4},{7,5},{8,10},{9,11},{10,... | collective-permute-start | bytes 147464 | tf_op jit(solution)/shard_map/ppermute | solution.py:106
  225.3 7.0 %collective-permute-start.2 = (f32[8,1536]{1,0:T(8,128)S(1)}, f32[8,1536]{1,0:T(8,128)S(1)}, u32[]{:S(2)}, u32[]{:S(2)}) collective-permute-start(f32[8,1536]{1,0:T(8,128)S(1)} %reduce_sum.19), channel_id=1, source_target_pairs={{0,3},{1,0},{2,1},{3,2},{4,7},{5,4},{6,5},{7,6},{8,11},{9,8},{10,9... | collective-permute-start | bytes 147464 | tf_op jit(solution)/shard_map/ppermute | solution.py:106
